TPU v7x, 1024 devices: a whole 4x8x16 slice. The times are simulated.
1024 devices in a mesh: seq: 64 (over z_lo, y), head: 8 (over z_hi, x), fsdp: 2 (over core).
Axes of the slice: x: 4, y: 8, z: 16 (z_hi: 2, z_lo: 8; z = z_hi * 8 + z_lo), core: 2. Of those that a mesh axis runs over, the one named last changes fastest.
Arguments:
- query: bfloat16 [2, 8192, 2048], P('fsdp', 'seq', 'head'), may hold values from -6 to 6
- keys: bfloat16 [2, 8192, 2048], P('fsdp', 'seq', 'head'), may hold values from -6 to 6
- values: bfloat16 [2, 8192, 2048], P('fsdp', 'seq', 'head'), may hold values from -6 to 6
- grad_out: bfloat16 [2, 8192, 4096], P('fsdp', 'seq'), may hold values from -16 to 16
- w_out: bfloat16 [2048, 4096], P('head', 'fsdp'), may hold values from -0.125 to 0.125
- link_flags: int32 [64, 6], P('seq'), may hold values 0 or 1
Outputs:
- grad_query: bfloat16 [2, 8192, 2048], P('fsdp', 'seq', 'head')
- grad_keys: bfloat16 [2, 8192, 2048], P('fsdp', 'seq', 'head')
- grad_values: bfloat16 [2, 8192, 2048], P('fsdp', 'seq', 'head')
- grad_w_out_t: float32 [4096, 2048], P('seq', ('head', 'fsdp'))
All inputs are finite; a program needn't handle non-finite values. No bound on the sum of `link_flags` on one device may be relied on, other than what follows from the above.
Results may differ from a plain program's by a relative error of at most 0.01.
Values may be sent and summed in bfloat16 or wider, within the bound.
No kernel may reach another device: no remote copies, remote signals or barrier semaphores. Data moves between devices by JAX's collectives and lax.ppermute only.
A program may use at most 32 MiB of HBM per device.

v0:
```python
import math

import jax
import jax.numpy as jnp
from jax import lax
from jax.sharding import PartitionSpec as P

D = 4096
HD = 128


def swapped(shard, axis, distance):
    return lax.ppermute(shard, axis, [(i, i ^ 1 << distance) for i in range(lax.axis_size(axis))])


def per_device(query, keys, values, grad_out, w_out, link_flags):
    local_seqs, block_len, local_width = query.shape
    local_heads = local_width // HD
    levels = lax.axis_size("seq").bit_length() - 1
    score_scale = 1.0 / math.sqrt(HD)
    key_value = jnp.stack([keys, values])
    collected = [key_value]
    for level in range(levels):
        collected.append(swapped(key_value, "seq", level))
    slots = levels + 1
    near_all = jnp.stack(collected).reshape(slots, 2, local_seqs, block_len, local_heads, HD)
    key_near = near_all[:, 0]
    value_near = near_all[:, 1]
    query_heads = query.reshape(local_seqs, block_len, local_heads, HD)
    spots = jnp.arange(block_len, dtype=jnp.int32)
    causal = spots[None, :] <= spots[:, None]
    link_on = jnp.concatenate([jnp.ones((1,), dtype=bool), link_flags[0] > 0])
    first_slot = jnp.arange(slots, dtype=jnp.int32) == 0
    allowed = jnp.where(first_slot[None, :, None], causal[:, None, :], link_on[None, :, None])
    scores = (
        jnp.einsum("sthc,msuhc->shtmu", query_heads, key_near, preferred_element_type=jnp.float32)
        * score_scale
    )
    scores = jnp.where(allowed[None, None], scores, -jnp.inf)
    row_max = jnp.max(scores, axis=(3, 4), keepdims=True)
    raw = jnp.exp(scores - row_max)
    softmax = raw / jnp.sum(raw, axis=(3, 4), keepdims=True)
    probs_low = softmax.astype(jnp.bfloat16)
    attended = jnp.einsum(
        "shtmu,msuhc->sthc", probs_low, value_near, preferred_element_type=jnp.float32
    ).astype(jnp.bfloat16)
    grad_rows = grad_out.reshape(local_seqs * block_len, D)
    columns = grad_rows
    grad_att = lax.dot_general(
        columns,
        lax.all_gather(w_out, "fsdp", axis=1, tiled=True),
        (((1,), (1,)), ((), ())),
        preferred_element_type=jnp.float32,
    ).astype(jnp.bfloat16)
    grad_heads = grad_att.reshape(local_seqs, block_len, local_heads, HD)
    attended_rows = attended.reshape(local_seqs * block_len, local_width)
    columns = grad_rows
    seq_share = lax.psum_scatter(
        lax.dot_general(
            columns, attended_rows, (((0,), (0,)), ((), ())), preferred_element_type=jnp.float32
        ),
        "seq",
        scatter_dimension=0,
        tiled=True,
    )
    grad_w = lax.psum_scatter(
        seq_share.astype(jnp.bfloat16), "fsdp", scatter_dimension=1, tiled=True
    ).astype(jnp.float32)
    grad_probs = jnp.einsum(
        "sthc,msuhc->shtmu", grad_heads, value_near, preferred_element_type=jnp.float32
    )
    row_dot = jnp.sum(softmax * grad_probs, axis=(3, 4), keepdims=True)
    grad_scores = (softmax * (grad_probs - row_dot) * score_scale).astype(jnp.bfloat16)
    grad_query = jnp.einsum(
        "shtmu,msuhc->sthc", grad_scores, key_near, preferred_element_type=jnp.float32
    ).astype(jnp.bfloat16)
    key_terms = jnp.einsum(
        "shtmu,sthc->msuhc", grad_scores, query_heads, preferred_element_type=jnp.float32
    )
    value_terms = jnp.einsum(
        "shtmu,sthc->msuhc", probs_low, grad_heads, preferred_element_type=jnp.float32
    )
    grad_key = key_terms[0]
    grad_value = value_terms[0]
    for level in range(levels):
        outgoing = jnp.stack([key_terms[level + 1], value_terms[level + 1]]).astype(jnp.bfloat16)
        returned = swapped(outgoing, "seq", level)
        grad_key = grad_key + returned[0].astype(jnp.float32)
        grad_value = grad_value + returned[1].astype(jnp.float32)
    shape_out = (local_seqs, block_len, local_width)
    return (
        grad_query.reshape(shape_out),
        grad_key.astype(jnp.bfloat16).reshape(shape_out),
        grad_value.astype(jnp.bfloat16).reshape(shape_out),
        grad_w,
    )


def solution(mesh):
    in_specs = (
        P("fsdp", "seq", "head"),
        P("fsdp", "seq", "head"),
        P("fsdp", "seq", "head"),
        P("fsdp", "seq", None),
        P("head", "fsdp"),
        P("seq", None),
    )
    out_specs = (
        P("fsdp", "seq", "head"),
        P("fsdp", "seq", "head"),
        P("fsdp", "seq", "head"),
        P("seq", ("head", "fsdp")),
    )
    return jax.shard_map(
        per_device, mesh=mesh, in_specs=in_specs, out_specs=out_specs, check_vma=False
    )
```

profile of v0, /device:TPU:1, one launch (start us, length us, event | category | flops | bytes accessed | tf_op | source)
XLA Modules:
  0.0 561.9 jit_solution(4095293683935275831)
XLA Ops:
  8.1 1.0 copy.50
  10.1 11.5 %collective-permute-start.5 = (bf16[2,1,128,256]{2,3,0,1:T(8,128)(2,1)S(1)}, bf16[2,1,128,256]{2,3,0,1:T(8,128)(2,1)S(1)}, u32[]{:S(2)}, u32[]{:S(2)}) collective-permute-start(bf16[2,1,128,256]{2,3,0,1:T(8,128)(2,1)S(1)} %pad_maximum_fusion), channel_id=1, source_target_pairs={{0,512},{16,528},{32,544},{48,560},{64,576},{80,592},{96,608},{112... | collective-permute-start | bytes 393224 | tf_op jit(solution)/shard_map/ppermute | solution.py:13
  21.5 5.8 %collective-permute-start.4 = (bf16[2,1,128,256]{2,3,0,1:T(8,128)(2,1)S(1)}, bf16[2,1,128,256]{2,3,0,1:T(8,128)(2,1)S(1)}, u32[]{:S(2)}, u32[]{:S(2)}) collective-permute-start(bf16[2,1,128,256]{2,3,0,1:T(8,128)(2,1)S(1)} %pad_maximum_fusion), channel_id=1, source_target_pairs={{0,256},{16,272},{32,288},{48,304},{64,320},{80,336},{96,352},{112... | collective-permute-start | bytes 393224 | tf_op jit(solution)/shard_map/ppermute | solution.py:13
  27.4 4.0 collective-permute-start.3
  31.4 7.5 %collective-permute-start.2 = (bf16[2,1,128,256]{2,3,0,1:T(8,128)(2,1)S(1)}, bf16[2,1,128,256]{2,3,0,1:T(8,128)(2,1)S(1)}, u32[]{:S(2)}, u32[]{:S(2)}) collective-permute-start(bf16[2,1,128,256]{2,3,0,1:T(8,128)(2,1)S(1)} %pad_maximum_fusion), channel_id=1, source_target_pairs={{0,64},{16,80},{32,96},{48,112},{64,0},{80,16},{96,32},{112,48},{1... | collective-permute-start | bytes 393224 | tf_op jit(solution)/shard_map/ppermute | solution.py:13
  38.8 2.4 collective-permute-start.1
  42.1 2.3 collective-permute-start
  46.4 5.5 collective-permute-done.1
  53.1 2.7 convolution_bitcast_fusion
  55.8 5.7 %copy.93 = f32[4096,256]{1,0:T(8,128)} copy(f32[4096,256]{0,1:T(8,128)} %convolution_bitcast_fusion) | data formatting | bytes 8388608
  61.6 4.9 all-gather.2.cloned.1.call-done
  66.4 2.4 convolution_convert_fusion
  68.9 1.3 fusion.33
  71.3 1.9 collective-permute-start.7
  73.9 4.9 collective-permute-start.8
  79.6 3.3 collective-permute-start.9
  83.5 4.3 collective-permute-start.10
  88.5 7.7 %collective-permute-start.11 = (bf16[2,1,128,2,128]{2,4,0,3,1:T(8,128)(2,1)}, bf16[2,1,128,2,128]{2,4,0,3,1:T(8,128)(2,1)S(1)}, u32[]{:S(2)}, u32[]{:S(2)}) collective-permute-start(bf16[2,1,128,2,128]{2,4,0,3,1:T(8,128)(2,1)} %pad_maximum_fusion.6), channel_id=1, source_target_pairs={{0,512},{16,528},{32,544},{48,560},{64,576},{80,592},{96,608},{112... | collective-permute-start | bytes 393224 | tf_op jit(solution)/shard_map/ppermute | solution.py:13
  96.9 2.2 collective-permute-start.6
  100.2 387.1 %reduce-scatter.7.cloned.1.call-done = f32[64,256]{1,0:T(8,128)} async-done(((f32[4096,256]{1,0:T(8,128)}), f32[64,256]{1,0:T(8,128)}) %reduce-scatter.7.cloned.1.call-update) | async-done | bytes 65552
  487.3 1.6 copy.94
  488.9 1.1 fusion.16
  491.6 61.4 %reduce-scatter.5.cloned.1.call-done = bf16[64,128]{0,1:T(8,128)(2,1)} async-done(((bf16[64,256]{0,1:T(8,128)(2,1)}), bf16[64,128]{0,1:T(8,128)(2,1)}) %reduce-scatter.5.cloned.1.call-update) | async-done | bytes 16400 | tf_op jit(solution)/shard_map/reduce_scatter | solution.py:66
  553.0 1.5 copy.75
  (63 shorter events, 12.1 us)
Async XLA Ops:
  8.0 45.1 %copy-start = (bf16[1,128,4096]{2,1,0:T(8,128)(2,1)S(1)}, bf16[1,128,4096]{2,1,0:T(8,128)(2,1)}, u32[]{:S(2)}) copy-start(bf16[1,128,4096]{2,1,0:T(8,128)(2,1)} %param.9) | copy-start | bytes 3145732
  8.0 58.4 %all-gather.2.cloned.1.call-start = ((), (), s32[]{:S(2)}) async-start(), calls=%async_computation.2 | async-start | bytes 3145728 | tf_op jit(solution)/shard_map/all_gather | solution.py:51
  10.1 32.0 %collective-permute-start.5 = (bf16[2,1,128,256]{2,3,0,1:T(8,128)(2,1)S(1)}, bf16[2,1,128,256]{2,3,0,1:T(8,128)(2,1)S(1)}, u32[]{:S(2)}, u32[]{:S(2)}) collective-permute-start(bf16[2,1,128,256]{2,3,0,1:T(8,128)(2,1)S(1)} %pad_maximum_fusion), channel_id=1, source_target_pairs={{0,512},{16,528},{32,544},{48,560},{64,576},{80,592},{96,608},{112... | collective-permute-start | bytes 393224 | tf_op jit(solution)/shard_map/ppermute | solution.py:13
  21.5 24.4 %collective-permute-start.4 = (bf16[2,1,128,256]{2,3,0,1:T(8,128)(2,1)S(1)}, bf16[2,1,128,256]{2,3,0,1:T(8,128)(2,1)S(1)}, u32[]{:S(2)}, u32[]{:S(2)}) collective-permute-start(bf16[2,1,128,256]{2,3,0,1:T(8,128)(2,1)S(1)} %pad_maximum_fusion), channel_id=1, source_target_pairs={{0,256},{16,272},{32,288},{48,304},{64,320},{80,336},{96,352},{112... | collective-permute-start | bytes 393224 | tf_op jit(solution)/shard_map/ppermute | solution.py:13
  27.4 18.7 %collective-permute-start.3 = (bf16[2,1,128,256]{2,3,0,1:T(8,128)(2,1)S(1)}, bf16[2,1,128,256]{2,3,0,1:T(8,128)(2,1)S(1)}, u32[]{:S(2)}, u32[]{:S(2)}) collective-permute-start(bf16[2,1,128,256]{2,3,0,1:T(8,128)(2,1)S(1)} %pad_maximum_fusion), channel_id=1, source_target_pairs={{0,128},{16,144},{32,160},{48,176},{64,192},{80,208},{96,224},{112... | collective-permute-start | bytes 393224 | tf_op jit(solution)/shard_map/ppermute | solution.py:13
  31.4 14.9 %collective-permute-start.2 = (bf16[2,1,128,256]{2,3,0,1:T(8,128)(2,1)S(1)}, bf16[2,1,128,256]{2,3,0,1:T(8,128)(2,1)S(1)}, u32[]{:S(2)}, u32[]{:S(2)}) collective-permute-start(bf16[2,1,128,256]{2,3,0,1:T(8,128)(2,1)S(1)} %pad_maximum_fusion), channel_id=1, source_target_pairs={{0,64},{16,80},{32,96},{48,112},{64,0},{80,16},{96,32},{112,48},{1... | collective-permute-start | bytes 393224 | tf_op jit(solution)/shard_map/ppermute | solution.py:13
  38.8 13.0 %collective-permute-start.1 = (bf16[2,1,128,256]{2,3,0,1:T(8,128)(2,1)S(1)}, bf16[2,1,128,256]{2,3,0,1:T(8,128)(2,1)S(1)}, u32[]{:S(2)}, u32[]{:S(2)}) collective-permute-start(bf16[2,1,128,256]{2,3,0,1:T(8,128)(2,1)S(1)} %pad_maximum_fusion), channel_id=1, source_target_pairs={{0,32},{16,48},{32,0},{48,16},{64,96},{80,112},{96,64},{112,80},{1... | collective-permute-start | bytes 393224 | tf_op jit(solution)/shard_map/ppermute | solution.py:13
  41.3 446.0 %reduce-scatter.7.cloned.1.call-start = ((), (), s32[]{:S(2)}) async-start(), calls=%async_computation.4 | async-start | bytes 4259840
  42.1 9.9 %collective-permute-start = (bf16[2,1,128,256]{2,3,0,1:T(8,128)(2,1)S(1)}, bf16[2,1,128,256]{2,3,0,1:T(8,128)(2,1)S(1)}, u32[]{:S(2)}, u32[]{:S(2)}) collective-permute-start(bf16[2,1,128,256]{2,3,0,1:T(8,128)(2,1)S(1)} %pad_maximum_fusion), channel_id=1, source_target_pairs={{0,16},{16,0},{32,48},{48,32},{64,80},{80,64},{96,112},{112,96},{1... | collective-permute-start | bytes 393224 | tf_op jit(solution)/shard_map/ppermute | solution.py:13
  61.5 491.5 %reduce-scatter.5.cloned.1.call-start = ((), (), s32[]{:S(2)}) async-start(), calls=%async_computation.3 | async-start | bytes 98304 | tf_op jit(solution)/shard_map/reduce_scatter | solution.py:66
  71.3 25.6 %collective-permute-start.7 = (bf16[2,1,128,2,128]{2,4,0,3,1:T(8,128)(2,1)S(1)}, bf16[2,1,128,2,128]{2,4,0,3,1:T(8,128)(2,1)S(1)}, u32[]{:S(2)}, u32[]{:S(2)}) collective-permute-start(bf16[2,1,128,2,128]{2,4,0,3,1:T(8,128)(2,1)S(1)} %pad_maximum_fusion.2), channel_id=1, source_target_pairs={{0,32},{16,48},{32,0},{48,16},{64,96},{80,112},{96,64},{112,80},{1... | collective-permute-start | bytes 393224 | tf_op jit(solution)/shard_map/ppermute | solution.py:13
  73.9 415.0 %collective-permute-start.8 = (bf16[2,1,128,2,128]{2,4,0,3,1:T(8,128)(2,1)}, bf16[2,1,128,2,128]{2,4,0,3,1:T(8,128)(2,1)S(1)}, u32[]{:S(2)}, u32[]{:S(2)}) collective-permute-start(bf16[2,1,128,2,128]{2,4,0,3,1:T(8,128)(2,1)} %pad_maximum_fusion.3), channel_id=1, source_target_pairs={{0,64},{16,80},{32,96},{48,112},{64,0},{80,16},{96,32},{112,48},{1... | collective-permute-start | bytes 393224 | tf_op jit(solution)/shard_map/ppermute | solution.py:13
  79.6 409.4 %collective-permute-start.9 = (bf16[2,1,128,2,128]{2,4,0,3,1:T(8,128)(2,1)}, bf16[2,1,128,2,128]{2,4,0,3,1:T(8,128)(2,1)S(1)}, u32[]{:S(2)}, u32[]{:S(2)}) collective-permute-start(bf16[2,1,128,2,128]{2,4,0,3,1:T(8,128)(2,1)} %pad_maximum_fusion.4), channel_id=1, source_target_pairs={{0,128},{16,144},{32,160},{48,176},{64,192},{80,208},{96,224},{112... | collective-permute-start | bytes 393224 | tf_op jit(solution)/shard_map/ppermute | solution.py:13
  83.5 405.4 %collective-permute-start.10 = (bf16[2,1,128,2,128]{2,4,0,3,1:T(8,128)(2,1)}, bf16[2,1,128,2,128]{2,4,0,3,1:T(8,128)(2,1)}, u32[]{:S(2)}, u32[]{:S(2)}) collective-permute-start(bf16[2,1,128,2,128]{2,4,0,3,1:T(8,128)(2,1)} %pad_maximum_fusion.5), channel_id=1, source_target_pairs={{0,256},{16,272},{32,288},{48,304},{64,320},{80,336},{96,352},{112... | collective-permute-start | bytes 393224 | tf_op jit(solution)/shard_map/ppermute | solution.py:13
  88.5 400.4 %collective-permute-start.11 = (bf16[2,1,128,2,128]{2,4,0,3,1:T(8,128)(2,1)}, bf16[2,1,128,2,128]{2,4,0,3,1:T(8,128)(2,1)S(1)}, u32[]{:S(2)}, u32[]{:S(2)}) collective-permute-start(bf16[2,1,128,2,128]{2,4,0,3,1:T(8,128)(2,1)} %pad_maximum_fusion.6), channel_id=1, source_target_pairs={{0,512},{16,528},{32,544},{48,560},{64,576},{80,592},{96,608},{112... | collective-permute-start | bytes 393224 | tf_op jit(solution)/shard_map/ppermute | solution.py:13
  96.9 392.0 %collective-permute-start.6 = (bf16[2,1,128,2,128]{2,4,0,3,1:T(8,128)(2,1)}, bf16[2,1,128,2,128]{2,4,0,3,1:T(8,128)(2,1)}, u32[]{:S(2)}, u32[]{:S(2)}) collective-permute-start(bf16[2,1,128,2,128]{2,4,0,3,1:T(8,128)(2,1)} %pad_maximum_fusion.1), channel_id=1, source_target_pairs={{0,16},{16,0},{32,48},{48,32},{64,80},{80,64},{96,112},{112,96},{1... | collective-permute-start | bytes 393224 | tf_op jit(solution)/shard_map/ppermute | solution.py:13
Sparse Core Ops, SparseCore 0:
  41.4 24.9 all-gather.1
  489.0 63.9 reduce-scatter.4
Sparse Core Ops, SparseCore 1:
  61.6 425.7 reduce-scatter.6
where the time goes:
time: 563 us; the launch traced here: 562 us
  waiting for transfers between devices  459 us (82%)
  starting transfers between devices  57.9 us (10%)
  between operations  15.9 us (3%)
  local copies, waits for them, and re-layouts  15.1 us (3%)
  matrix products  7.96 us (1%)
  other arithmetic  6.05 us (1%)
    unnamed x4, waiting for transfers between devices  387 us
    reduce_scatter x1, waiting for transfers between devices, per_device(): lax.psum_scatter(seq_share.astype(jnp.bfloat16), 'fsdp', scatter_dimensio...  61.4 us
    ppermute x12, starting transfers between devices, swapped(): lax.ppermute(shard, axis, [(i, i ^ 1 << distance) for i in range(lax.axis...  57.8 us
    unnamed x15, local copies, waits for them, and re-layouts  13 us
  transfers between devices with their start and end apart: 15, of which 4 were waited for; matrix products, arithmetic and copies ran while one was open for 5% of the time, Pallas kernels for 0%

commit v1 on v0

--- a/solution.py
+++ b/solution.py
@@ -11,6 +11,29 @@
 
 def swapped(shard, axis, distance):
     return lax.ppermute(shard, axis, [(i, i ^ 1 << distance) for i in range(lax.axis_size(axis))])
+
+
+def halving_scatter(partial, axis, levels):
+    rows, cols = partial.shape
+    here = lax.axis_index(axis)
+    block = rows >> levels
+    pieces = partial.reshape((2,) * levels + (2, block // 2, cols))
+    low = [b for b in range(levels) if b < (levels + 1) // 2]
+    high = [b for b in range(levels) if b >= (levels + 1) // 2]
+    first = [b for pair in zip(low, high) for b in pair] + low[len(high):]
+    second = [b for pair in zip(high, low) for b in pair] + low[len(high):]
+    halves = [pieces[..., 0, :, :], pieces[..., 1, :, :]]
+    bits_left = [list(range(levels - 1, -1, -1)), list(range(levels - 1, -1, -1))]
+    for step in range(levels):
+        for h, order in enumerate((first, second)):
+            bit = order[step]
+            at = bits_left[h].index(bit)
+            mine = (here >> bit) & 1
+            keep = lax.dynamic_index_in_dim(halves[h], mine, at, keepdims=False)
+            send = lax.dynamic_index_in_dim(halves[h], 1 - mine, at, keepdims=False)
+            halves[h] = keep + swapped(send, axis, bit)
+            bits_left[h].pop(at)
+    return jnp.concatenate(halves, axis=0)
 
 
 def per_device(query, keys, values, grad_out, w_out, link_flags):
@@ -45,6 +68,7 @@
         "shtmu,msuhc->sthc", probs_low, value_near, preferred_element_type=jnp.float32
     ).astype(jnp.bfloat16)
     grad_rows = grad_out.reshape(local_seqs * block_len, D)
+    grad_rows_other = swapped(grad_rows, "fsdp", 0)
     columns = grad_rows
     grad_att = lax.dot_general(
         columns,
@@ -54,18 +78,18 @@
     ).astype(jnp.bfloat16)
     grad_heads = grad_att.reshape(local_seqs, block_len, local_heads, HD)
     attended_rows = attended.reshape(local_seqs * block_len, local_width)
-    columns = grad_rows
-    seq_share = lax.psum_scatter(
-        lax.dot_general(
-            columns, attended_rows, (((0,), (0,)), ((), ())), preferred_element_type=jnp.float32
-        ),
-        "seq",
-        scatter_dimension=0,
-        tiled=True,
+    fsdp_size = lax.axis_size("fsdp")
+    fsdp_at = lax.axis_index("fsdp")
+    share = local_width // fsdp_size
+    own_cols = lax.dynamic_slice_in_dim(attended_rows, fsdp_at * share, share, axis=1)
+    given_cols = lax.dynamic_slice_in_dim(attended_rows, (1 - fsdp_at) * share, share, axis=1)
+    taken_cols = swapped(given_cols, "fsdp", 0)
+    token_rows = jnp.concatenate([grad_rows, grad_rows_other], axis=0)
+    token_cols = jnp.concatenate([own_cols, taken_cols], axis=0)
+    partial = lax.dot_general(
+        token_rows, token_cols, (((0,), (0,)), ((), ())), preferred_element_type=jnp.float32
     )
-    grad_w = lax.psum_scatter(
-        seq_share.astype(jnp.bfloat16), "fsdp", scatter_dimension=1, tiled=True
-    ).astype(jnp.float32)
+    grad_w = halving_scatter(partial, "seq", levels)
     grad_probs = jnp.einsum(
         "sthc,msuhc->shtmu", grad_heads, value_near, preferred_element_type=jnp.float32
     )

time: 563 us -> 172 us (0.31)
  the two profiles are of different devices: /device:TPU:1 before, /device:TPU:12 now
where the time goes in v1:
time: 172 us; the launch traced here: 171 us
  starting transfers between devices  101 us (59%)
  waiting for transfers between devices  33.8 us (20%)
  between operations  14.8 us (9%)
  local copies, waits for them, and re-layouts  10.5 us (6%)
  matrix products  6.35 us (4%)
  other arithmetic  4.92 us (3%)
    ppermute x26, starting transfers between devices, swapped(): lax.ppermute(shard, axis, [(i, i ^ 1 << distance) for i in range(lax.axis...  101 us
    ppermute x26, waiting for transfers between devices, swapped(): lax.ppermute(shard, axis, [(i, i ^ 1 << distance) for i in range(lax.axis...  33.8 us
    unnamed x18, local copies, waits for them, and re-layouts  5.28 us
  transfers between devices with their start and end apart: 27, of which 11 were waited for; matrix products, arithmetic and copies ran while one was open for 6% of the time, Pallas kernels for 0%

profile of v1, /device:TPU:12, one launch (start us, length us, event | category | flops | bytes accessed | tf_op | source)
XLA Modules:
  0.0 171.0 jit_solution(16438576973611527760)
XLA Ops:
  9.2 10.9 %collective-permute-start.5 = (bf16[2,1,128,256]{2,3,0,1:T(8,128)(2,1)S(1)}, bf16[2,1,128,256]{2,3,0,1:T(8,128)(2,1)S(1)}, u32[]{:S(2)}, u32[]{:S(2)}) collective-permute-start(bf16[2,1,128,256]{2,3,0,1:T(8,128)(2,1)S(1)} %pad_maximum_fusion), channel_id=1, source_target_pairs={{0,512},{16,528},{32,544},{48,560},{64,576},{80,592},{96,608},{112... | collective-permute-start | bytes 393224 | tf_op jit(solution)/shard_map/ppermute | solution.py:13
  20.1 6.1 %collective-permute-start.4 = (bf16[2,1,128,256]{2,3,0,1:T(8,128)(2,1)S(1)}, bf16[2,1,128,256]{2,3,0,1:T(8,128)(2,1)S(1)}, u32[]{:S(2)}, u32[]{:S(2)}) collective-permute-start(bf16[2,1,128,256]{2,3,0,1:T(8,128)(2,1)S(1)} %pad_maximum_fusion), channel_id=1, source_target_pairs={{0,256},{16,272},{32,288},{48,304},{64,320},{80,336},{96,352},{112... | collective-permute-start | bytes 393224 | tf_op jit(solution)/shard_map/ppermute | solution.py:13
  26.2 4.3 %collective-permute-start.3 = (bf16[2,1,128,256]{2,3,0,1:T(8,128)(2,1)S(1)}, bf16[2,1,128,256]{2,3,0,1:T(8,128)(2,1)S(1)}, u32[]{:S(2)}, u32[]{:S(2)}) collective-permute-start(bf16[2,1,128,256]{2,3,0,1:T(8,128)(2,1)S(1)} %pad_maximum_fusion), channel_id=1, source_target_pairs={{0,128},{16,144},{32,160},{48,176},{64,192},{80,208},{96,224},{112... | collective-permute-start | bytes 393224 | tf_op jit(solution)/shard_map/ppermute | solution.py:13
  30.5 6.8 %collective-permute-start.2 = (bf16[2,1,128,256]{2,3,0,1:T(8,128)(2,1)S(1)}, bf16[2,1,128,256]{2,3,0,1:T(8,128)(2,1)S(1)}, u32[]{:S(2)}, u32[]{:S(2)}) collective-permute-start(bf16[2,1,128,256]{2,3,0,1:T(8,128)(2,1)S(1)} %pad_maximum_fusion), channel_id=1, source_target_pairs={{0,64},{16,80},{32,96},{48,112},{64,0},{80,16},{96,32},{112,48},{1... | collective-permute-start | bytes 393224 | tf_op jit(solution)/shard_map/ppermute | solution.py:13
  37.3 2.7 %collective-permute-start.1 = (bf16[2,1,128,256]{2,3,0,1:T(8,128)(2,1)S(1)}, bf16[2,1,128,256]{2,3,0,1:T(8,128)(2,1)S(1)}, u32[]{:S(2)}, u32[]{:S(2)}) collective-permute-start(bf16[2,1,128,256]{2,3,0,1:T(8,128)(2,1)S(1)} %pad_maximum_fusion), channel_id=1, source_target_pairs={{0,32},{16,48},{32,0},{48,16},{64,96},{80,112},{96,64},{112,80},{1... | collective-permute-start | bytes 393224 | tf_op jit(solution)/shard_map/ppermute | solution.py:13
  40.8 3.3 %collective-permute-start = (bf16[2,1,128,256]{2,3,0,1:T(8,128)(2,1)S(1)}, bf16[2,1,128,256]{2,3,0,1:T(8,128)(2,1)S(1)}, u32[]{:S(2)}, u32[]{:S(2)}) collective-permute-start(bf16[2,1,128,256]{2,3,0,1:T(8,128)(2,1)S(1)} %pad_maximum_fusion), channel_id=1, source_target_pairs={{0,16},{16,0},{32,48},{48,32},{64,80},{80,64},{96,112},{112,96},{1... | collective-permute-start | bytes 393224 | tf_op jit(solution)/shard_map/ppermute | solution.py:13
  61.0 3.7 %collective-permute-start.14 = (f32[2,2,2,2,2,32,128]{6,5,4,3,2,1,0:T(8,128)}, f32[2,2,2,2,2,32,128]{6,5,4,3,2,1,0:T(8,128)}, u32[]{:S(2)}, u32[]{:S(2)}) collective-permute-start(f32[2,2,2,2,2,32,128]{6,5,4,3,2,1,0:T(8,128)} %dynamic-slice_bitcast_fusion.1), channel_id=1, source_target_pairs={{0,16},{16,0},{32,48},{48,32},{64,80},{80,64},{96,112},{112,96},{1... | collective-permute-start | bytes 1572872 | tf_op jit(solution)/shard_map/ppermute | solution.py:13
  65.8 8.3 %collective-permute-done.20 = f32[2,2,2,2,2,32,128]{6,5,4,3,2,1,0:T(8,128)} collective-permute-done((f32[2,2,2,2,2,32,128]{6,5,4,3,2,1,0:T(8,128)}, f32[2,2,2,2,2,32,128]{6,5,4,3,2,1,0:T(8,128)}, u32[]{:S(2)}, u32[]{:S(2)}) %collective-permute-start.20) | collective-permute-done | bytes 524320 | tf_op jit(solution)/shard_map/ppermute | solution.py:13
  75.4 3.8 %collective-permute-start.21 = (f32[2,2,2,2,32,128]{5,4,3,2,1,0:T(8,128)S(1)}, f32[2,2,2,2,32,128]{5,4,3,2,1,0:T(8,128)S(1)}, u32[]{:S(2)}, u32[]{:S(2)}) collective-permute-start(f32[2,2,2,2,32,128]{5,4,3,2,1,0:T(8,128)S(1)} %dynamic-slice_bitcast_fusion.2), channel_id=1, source_target_pairs={{0,16},{16,0},{32,48},{48,32},{64,80},{80,64},{96,112},{112,96},{1... | collective-permute-start | bytes 786440 | tf_op jit(solution)/shard_map/ppermute | solution.py:13
  82.6 2.4 %collective-permute-done.21 = f32[2,2,2,2,32,128]{5,4,3,2,1,0:T(8,128)S(1)} collective-permute-done((f32[2,2,2,2,32,128]{5,4,3,2,1,0:T(8,128)S(1)}, f32[2,2,2,2,32,128]{5,4,3,2,1,0:T(8,128)S(1)}, u32[]{:S(2)}, u32[]{:S(2)}) %collective-permute-start.21) | collective-permute-done | bytes 262176 | tf_op jit(solution)/shard_map/ppermute | solution.py:13
  87.2 2.8 %collective-permute-done.15 = f32[2,2,2,2,32,128]{5,4,3,2,1,0:T(8,128)S(1)} collective-permute-done((f32[2,2,2,2,32,128]{5,4,3,2,1,0:T(8,128)S(1)}, f32[2,2,2,2,32,128]{5,4,3,2,1,0:T(8,128)S(1)}, u32[]{:S(2)}, u32[]{:S(2)}) %collective-permute-start.15) | collective-permute-done | bytes 262176 | tf_op jit(solution)/shard_map/ppermute | solution.py:13
  90.0 2.6 %collective-permute-start.16 = (f32[2,2,2,32,128]{4,3,2,1,0:T(8,128)S(1)}, f32[2,2,2,32,128]{4,3,2,1,0:T(8,128)S(1)}, u32[]{:S(2)}, u32[]{:S(2)}) collective-permute-start(f32[2,2,2,32,128]{4,3,2,1,0:T(8,128)S(1)} %dynamic-slice_bitcast_fusion.5), channel_id=1, source_target_pairs={{0,32},{16,48},{32,0},{48,16},{64,96},{80,112},{96,64},{112,80},{1... | collective-permute-start | bytes 393224 | tf_op jit(solution)/shard_map/ppermute | solution.py:13
  94.5 4.5 %collective-permute-start.23 = (f32[2,2,32,128]{3,2,1,0:T(8,128)S(1)}, f32[2,2,32,128]{3,2,1,0:T(8,128)S(1)}, u32[]{:S(2)}, u32[]{:S(2)}) collective-permute-start(f32[2,2,32,128]{3,2,1,0:T(8,128)S(1)} %dynamic-slice_bitcast_fusion.6), channel_id=1, source_target_pairs={{0,32},{16,48},{32,0},{48,16},{64,96},{80,112},{96,64},{112,80},{1... | collective-permute-start | bytes 196616 | tf_op jit(solution)/shard_map/ppermute | solution.py:13
  99.1 2.7 %collective-permute-start.17 = (f32[2,2,32,128]{3,2,1,0:T(8,128)S(1)}, f32[2,2,32,128]{3,2,1,0:T(8,128)S(1)}, u32[]{:S(2)}, u32[]{:S(2)}) collective-permute-start(f32[2,2,32,128]{3,2,1,0:T(8,128)S(1)} %dynamic-slice_bitcast_fusion.7), channel_id=1, source_target_pairs={{0,256},{16,272},{32,288},{48,304},{64,320},{80,336},{96,352},{112... | collective-permute-start | bytes 196616 | tf_op jit(solution)/shard_map/ppermute | solution.py:13
  106.2 3.8 %collective-permute-start.18 = (f32[2,32,128]{2,1,0:T(8,128)S(1)}, f32[2,32,128]{2,1,0:T(8,128)S(1)}, u32[]{:S(2)}, u32[]{:S(2)}) collective-permute-start(f32[2,32,128]{2,1,0:T(8,128)S(1)} %dynamic-slice_bitcast_fusion.9), channel_id=1, source_target_pairs={{0,64},{16,80},{32,96},{48,112},{64,0},{80,16},{96,32},{112,48},{1... | collective-permute-start | bytes 98312 | tf_op jit(solution)/shard_map/ppermute | solution.py:13
  111.9 4.1 %collective-permute-start.25 = (f32[32,128]{1,0:T(8,128)S(1)}, f32[32,128]{1,0:T(8,128)S(1)}, u32[]{:S(2)}, u32[]{:S(2)}) collective-permute-start(f32[32,128]{1,0:T(8,128)S(1)} %dynamic-slice_bitcast_fusion.10), channel_id=1, source_target_pairs={{0,64},{16,80},{32,96},{48,112},{64,0},{80,16},{96,32},{112,48},{1... | collective-permute-start | bytes 49160 | tf_op jit(solution)/shard_map/ppermute | solution.py:13
  116.0 5.5 %collective-permute-start.19 = (f32[32,128]{1,0:T(8,128)S(1)}, f32[32,128]{1,0:T(8,128)S(1)}, u32[]{:S(2)}, u32[]{:S(2)}) collective-permute-start(f32[32,128]{1,0:T(8,128)S(1)} %dynamic-slice_bitcast_fusion.11), channel_id=1, source_target_pairs={{0,512},{16,528},{32,544},{48,560},{64,576},{80,592},{96,608},{112... | collective-permute-start | bytes 49160 | tf_op jit(solution)/shard_map/ppermute | solution.py:13
  121.6 4.0 %collective-permute-done.19 = f32[32,128]{1,0:T(8,128)S(1)} collective-permute-done((f32[32,128]{1,0:T(8,128)S(1)}, f32[32,128]{1,0:T(8,128)S(1)}, u32[]{:S(2)}, u32[]{:S(2)}) %collective-permute-start.19) | collective-permute-done | bytes 16416 | tf_op jit(solution)/shard_map/ppermute | solution.py:13
  126.2 2.4 %convolution_convert_fusion = bf16[128,256]{1,0:T(8,128)(2,1)S(1)} fusion(bf16[256,4096]{1,0:T(8,128)(2,1)} %all-gather.2.cloned.1.call-done, bf16[1,128,4096]{2,1,0:T(8,128)(2,1)S(1)} %copy-done), kind=kOutput, calls=%fused_computation.11 | convolution fusion | flops 268468224 | bytes 3211264 | tf_op jit(solution)/shard_map/dot_general | solution.py:73
  130.2 4.3 %collective-permute-start.7 = (bf16[2,1,128,2,128]{2,4,0,3,1:T(8,128)(2,1)S(1)}, bf16[2,1,128,2,128]{2,4,0,3,1:T(8,128)(2,1)S(1)}, u32[]{:S(2)}, u32[]{:S(2)}) collective-permute-start(bf16[2,1,128,2,128]{2,4,0,3,1:T(8,128)(2,1)S(1)} %pad_maximum_fusion.2), channel_id=1, source_target_pairs={{0,32},{16,48},{32,0},{48,16},{64,96},{80,112},{96,64},{112,80},{1... | collective-permute-start | bytes 393224 | tf_op jit(solution)/shard_map/ppermute | solution.py:13
  134.4 6.6 %collective-permute-start.8 = (bf16[2,1,128,2,128]{2,4,0,3,1:T(8,128)(2,1)S(1)}, bf16[2,1,128,2,128]{2,4,0,3,1:T(8,128)(2,1)S(1)}, u32[]{:S(2)}, u32[]{:S(2)}) collective-permute-start(bf16[2,1,128,2,128]{2,4,0,3,1:T(8,128)(2,1)S(1)} %pad_maximum_fusion.3), channel_id=1, source_target_pairs={{0,64},{16,80},{32,96},{48,112},{64,0},{80,16},{96,32},{112,48},{1... | collective-permute-start | bytes 393224 | tf_op jit(solution)/shard_map/ppermute | solution.py:13
  143.4 4.7 %collective-permute-start.10 = (bf16[2,1,128,2,128]{2,4,0,3,1:T(8,128)(2,1)S(1)}, bf16[2,1,128,2,128]{2,4,0,3,1:T(8,128)(2,1)S(1)}, u32[]{:S(2)}, u32[]{:S(2)}) collective-permute-start(bf16[2,1,128,2,128]{2,4,0,3,1:T(8,128)(2,1)S(1)} %pad_maximum_fusion.5), channel_id=1, source_target_pairs={{0,256},{16,272},{32,288},{48,304},{64,320},{80,336},{96,352},{112... | collective-permute-start | bytes 393224 | tf_op jit(solution)/shard_map/ppermute | solution.py:13
  148.2 3.7 %collective-permute-start.11 = (bf16[2,1,128,2,128]{2,4,0,3,1:T(8,128)(2,1)S(1)}, bf16[2,1,128,2,128]{2,4,0,3,1:T(8,128)(2,1)S(1)}, u32[]{:S(2)}, u32[]{:S(2)}) collective-permute-start(bf16[2,1,128,2,128]{2,4,0,3,1:T(8,128)(2,1)S(1)} %pad_maximum_fusion.6), channel_id=1, source_target_pairs={{0,512},{16,528},{32,544},{48,560},{64,576},{80,592},{96,608},{112... | collective-permute-start | bytes 393224 | tf_op jit(solution)/shard_map/ppermute | solution.py:13
  154.9 7.7 %collective-permute-done.11 = bf16[2,1,128,2,128]{2,4,0,3,1:T(8,128)(2,1)S(1)} collective-permute-done((bf16[2,1,128,2,128]{2,4,0,3,1:T(8,128)(2,1)S(1)}, bf16[2,1,128,2,128]{2,4,0,3,1:T(8,128)(2,1)S(1)}, u32[]{:S(2)}, u32[]{:S(2)}) %collective-permute-start.11) | collective-permute-done | bytes 131104 | tf_op jit(solution)/shard_map/ppermute | solution.py:13
  (115 shorter events, 44.7 us)
Async XLA Ops:
  7.2 119.0 %all-gather.2.cloned.1.call-start = ((), (), s32[]{:S(2)}) async-start(), calls=%async_computation | async-start | bytes 3145728 | tf_op jit(solution)/shard_map/all_gather | solution.py:75
  9.2 31.6 %collective-permute-start.5 = (bf16[2,1,128,256]{2,3,0,1:T(8,128)(2,1)S(1)}, bf16[2,1,128,256]{2,3,0,1:T(8,128)(2,1)S(1)}, u32[]{:S(2)}, u32[]{:S(2)}) collective-permute-start(bf16[2,1,128,256]{2,3,0,1:T(8,128)(2,1)S(1)} %pad_maximum_fusion), channel_id=1, source_target_pairs={{0,512},{16,528},{32,544},{48,560},{64,576},{80,592},{96,608},{112... | collective-permute-start | bytes 393224 | tf_op jit(solution)/shard_map/ppermute | solution.py:13
  20.1 25.5 %collective-permute-start.4 = (bf16[2,1,128,256]{2,3,0,1:T(8,128)(2,1)S(1)}, bf16[2,1,128,256]{2,3,0,1:T(8,128)(2,1)S(1)}, u32[]{:S(2)}, u32[]{:S(2)}) collective-permute-start(bf16[2,1,128,256]{2,3,0,1:T(8,128)(2,1)S(1)} %pad_maximum_fusion), channel_id=1, source_target_pairs={{0,256},{16,272},{32,288},{48,304},{64,320},{80,336},{96,352},{112... | collective-permute-start | bytes 393224 | tf_op jit(solution)/shard_map/ppermute | solution.py:13
  26.2 21.5 %collective-permute-start.3 = (bf16[2,1,128,256]{2,3,0,1:T(8,128)(2,1)S(1)}, bf16[2,1,128,256]{2,3,0,1:T(8,128)(2,1)S(1)}, u32[]{:S(2)}, u32[]{:S(2)}) collective-permute-start(bf16[2,1,128,256]{2,3,0,1:T(8,128)(2,1)S(1)} %pad_maximum_fusion), channel_id=1, source_target_pairs={{0,128},{16,144},{32,160},{48,176},{64,192},{80,208},{96,224},{112... | collective-permute-start | bytes 393224 | tf_op jit(solution)/shard_map/ppermute | solution.py:13
  30.5 17.4 %collective-permute-start.2 = (bf16[2,1,128,256]{2,3,0,1:T(8,128)(2,1)S(1)}, bf16[2,1,128,256]{2,3,0,1:T(8,128)(2,1)S(1)}, u32[]{:S(2)}, u32[]{:S(2)}) collective-permute-start(bf16[2,1,128,256]{2,3,0,1:T(8,128)(2,1)S(1)} %pad_maximum_fusion), channel_id=1, source_target_pairs={{0,64},{16,80},{32,96},{48,112},{64,0},{80,16},{96,32},{112,48},{1... | collective-permute-start | bytes 393224 | tf_op jit(solution)/shard_map/ppermute | solution.py:13
  37.3 11.1 %collective-permute-start.1 = (bf16[2,1,128,256]{2,3,0,1:T(8,128)(2,1)S(1)}, bf16[2,1,128,256]{2,3,0,1:T(8,128)(2,1)S(1)}, u32[]{:S(2)}, u32[]{:S(2)}) collective-permute-start(bf16[2,1,128,256]{2,3,0,1:T(8,128)(2,1)S(1)} %pad_maximum_fusion), channel_id=1, source_target_pairs={{0,32},{16,48},{32,0},{48,16},{64,96},{80,112},{96,64},{112,80},{1... | collective-permute-start | bytes 393224 | tf_op jit(solution)/shard_map/ppermute | solution.py:13
  40.8 8.8 %collective-permute-start = (bf16[2,1,128,256]{2,3,0,1:T(8,128)(2,1)S(1)}, bf16[2,1,128,256]{2,3,0,1:T(8,128)(2,1)S(1)}, u32[]{:S(2)}, u32[]{:S(2)}) collective-permute-start(bf16[2,1,128,256]{2,3,0,1:T(8,128)(2,1)S(1)} %pad_maximum_fusion), channel_id=1, source_target_pairs={{0,16},{16,0},{32,48},{48,32},{64,80},{80,64},{96,112},{112,96},{1... | collective-permute-start | bytes 393224 | tf_op jit(solution)/shard_map/ppermute | solution.py:13
  45.6 8.3 %collective-permute-start.12 = (bf16[128,4096]{1,0:T(8,128)(2,1)}, bf16[128,4096]{1,0:T(8,128)(2,1)}, u32[]{:S(2)}, u32[]{:S(2)}) collective-permute-start(bf16[128,4096]{1,0:T(8,128)(2,1)} %bitcast.141), channel_id=1, source_target_pairs={{0,1},{1,0},{2,3},{3,2},{4,5},{5,4},{6,7},{7,6},{8,9},{9,8},{10,11... | collective-permute-start | bytes 3145736 | tf_op jit(solution)/shard_map/ppermute | solution.py:13
  57.9 16.2 %collective-permute-start.20 = (f32[2,2,2,2,2,32,128]{6,5,4,3,2,1,0:T(8,128)}, f32[2,2,2,2,2,32,128]{6,5,4,3,2,1,0:T(8,128)}, u32[]{:S(2)}, u32[]{:S(2)}) collective-permute-start(f32[2,2,2,2,2,32,128]{6,5,4,3,2,1,0:T(8,128)} %dynamic-slice_bitcast_fusion), channel_id=1, source_target_pairs={{0,128},{16,144},{32,160},{48,176},{64,192},{80,208},{96,224},{112... | collective-permute-start | bytes 1572872 | tf_op jit(solution)/shard_map/ppermute | solution.py:13
  61.0 18.2 %collective-permute-start.14 = (f32[2,2,2,2,2,32,128]{6,5,4,3,2,1,0:T(8,128)}, f32[2,2,2,2,2,32,128]{6,5,4,3,2,1,0:T(8,128)}, u32[]{:S(2)}, u32[]{:S(2)}) collective-permute-start(f32[2,2,2,2,2,32,128]{6,5,4,3,2,1,0:T(8,128)} %dynamic-slice_bitcast_fusion.1), channel_id=1, source_target_pairs={{0,16},{16,0},{32,48},{48,32},{64,80},{80,64},{96,112},{112,96},{1... | collective-permute-start | bytes 1572872 | tf_op jit(solution)/shard_map/ppermute | solution.py:13
  75.4 9.5 %collective-permute-start.21 = (f32[2,2,2,2,32,128]{5,4,3,2,1,0:T(8,128)S(1)}, f32[2,2,2,2,32,128]{5,4,3,2,1,0:T(8,128)S(1)}, u32[]{:S(2)}, u32[]{:S(2)}) collective-permute-start(f32[2,2,2,2,32,128]{5,4,3,2,1,0:T(8,128)S(1)} %dynamic-slice_bitcast_fusion.2), channel_id=1, source_target_pairs={{0,16},{16,0},{32,48},{48,32},{64,80},{80,64},{96,112},{112,96},{1... | collective-permute-start | bytes 786440 | tf_op jit(solution)/shard_map/ppermute | solution.py:13
  80.4 9.6 %collective-permute-start.15 = (f32[2,2,2,2,32,128]{5,4,3,2,1,0:T(8,128)S(1)}, f32[2,2,2,2,32,128]{5,4,3,2,1,0:T(8,128)S(1)}, u32[]{:S(2)}, u32[]{:S(2)}) collective-permute-start(f32[2,2,2,2,32,128]{5,4,3,2,1,0:T(8,128)S(1)} %dynamic-slice_bitcast_fusion.3), channel_id=1, source_target_pairs={{0,128},{16,144},{32,160},{48,176},{64,192},{80,208},{96,224},{112... | collective-permute-start | bytes 786440 | tf_op jit(solution)/shard_map/ppermute | solution.py:13
  85.0 9.4 %collective-permute-start.22 = (f32[2,2,2,32,128]{4,3,2,1,0:T(8,128)S(1)}, f32[2,2,2,32,128]{4,3,2,1,0:T(8,128)S(1)}, u32[]{:S(2)}, u32[]{:S(2)}) collective-permute-start(f32[2,2,2,32,128]{4,3,2,1,0:T(8,128)S(1)} %dynamic-slice_bitcast_fusion.4), channel_id=1, source_target_pairs={{0,256},{16,272},{32,288},{48,304},{64,320},{80,336},{96,352},{112... | collective-permute-start | bytes 393224 | tf_op jit(solution)/shard_map/ppermute | solution.py:13
  90.0 9.0 %collective-permute-start.16 = (f32[2,2,2,32,128]{4,3,2,1,0:T(8,128)S(1)}, f32[2,2,2,32,128]{4,3,2,1,0:T(8,128)S(1)}, u32[]{:S(2)}, u32[]{:S(2)}) collective-permute-start(f32[2,2,2,32,128]{4,3,2,1,0:T(8,128)S(1)} %dynamic-slice_bitcast_fusion.5), channel_id=1, source_target_pairs={{0,32},{16,48},{32,0},{48,16},{64,96},{80,112},{96,64},{112,80},{1... | collective-permute-start | bytes 393224 | tf_op jit(solution)/shard_map/ppermute | solution.py:13
  101.8 10.0 %collective-permute-start.24 = (f32[2,32,128]{2,1,0:T(8,128)S(1)}, f32[2,32,128]{2,1,0:T(8,128)S(1)}, u32[]{:S(2)}, u32[]{:S(2)}) collective-permute-start(f32[2,32,128]{2,1,0:T(8,128)S(1)} %dynamic-slice_bitcast_fusion.8), channel_id=1, source_target_pairs={{0,512},{16,528},{32,544},{48,560},{64,576},{80,592},{96,608},{112... | collective-permute-start | bytes 98312 | tf_op jit(solution)/shard_map/ppermute | solution.py:13
  106.2 9.8 %collective-permute-start.18 = (f32[2,32,128]{2,1,0:T(8,128)S(1)}, f32[2,32,128]{2,1,0:T(8,128)S(1)}, u32[]{:S(2)}, u32[]{:S(2)}) collective-permute-start(f32[2,32,128]{2,1,0:T(8,128)S(1)} %dynamic-slice_bitcast_fusion.9), channel_id=1, source_target_pairs={{0,64},{16,80},{32,96},{48,112},{64,0},{80,16},{96,32},{112,48},{1... | collective-permute-start | bytes 98312 | tf_op jit(solution)/shard_map/ppermute | solution.py:13
  111.9 9.7 %collective-permute-start.25 = (f32[32,128]{1,0:T(8,128)S(1)}, f32[32,128]{1,0:T(8,128)S(1)}, u32[]{:S(2)}, u32[]{:S(2)}) collective-permute-start(f32[32,128]{1,0:T(8,128)S(1)} %dynamic-slice_bitcast_fusion.10), channel_id=1, source_target_pairs={{0,64},{16,80},{32,96},{48,112},{64,0},{80,16},{96,32},{112,48},{1... | collective-permute-start | bytes 49160 | tf_op jit(solution)/shard_map/ppermute | solution.py:13
  116.0 9.5 %collective-permute-start.19 = (f32[32,128]{1,0:T(8,128)S(1)}, f32[32,128]{1,0:T(8,128)S(1)}, u32[]{:S(2)}, u32[]{:S(2)}) collective-permute-start(f32[32,128]{1,0:T(8,128)S(1)} %dynamic-slice_bitcast_fusion.11), channel_id=1, source_target_pairs={{0,512},{16,528},{32,544},{48,560},{64,576},{80,592},{96,608},{112... | collective-permute-start | bytes 49160 | tf_op jit(solution)/shard_map/ppermute | solution.py:13
  130.2 21.7 %collective-permute-start.7 = (bf16[2,1,128,2,128]{2,4,0,3,1:T(8,128)(2,1)S(1)}, bf16[2,1,128,2,128]{2,4,0,3,1:T(8,128)(2,1)S(1)}, u32[]{:S(2)}, u32[]{:S(2)}) collective-permute-start(bf16[2,1,128,2,128]{2,4,0,3,1:T(8,128)(2,1)S(1)} %pad_maximum_fusion.2), channel_id=1, source_target_pairs={{0,32},{16,48},{32,0},{48,16},{64,96},{80,112},{96,64},{112,80},{1... | collective-permute-start | bytes 393224 | tf_op jit(solution)/shard_map/ppermute | solution.py:13
  134.4 20.5 %collective-permute-start.8 = (bf16[2,1,128,2,128]{2,4,0,3,1:T(8,128)(2,1)S(1)}, bf16[2,1,128,2,128]{2,4,0,3,1:T(8,128)(2,1)S(1)}, u32[]{:S(2)}, u32[]{:S(2)}) collective-permute-start(bf16[2,1,128,2,128]{2,4,0,3,1:T(8,128)(2,1)S(1)} %pad_maximum_fusion.3), channel_id=1, source_target_pairs={{0,64},{16,80},{32,96},{48,112},{64,0},{80,16},{96,32},{112,48},{1... | collective-permute-start | bytes 393224 | tf_op jit(solution)/shard_map/ppermute | solution.py:13
  141.1 13.8 %collective-permute-start.9 = (bf16[2,1,128,2,128]{2,4,0,3,1:T(8,128)(2,1)S(1)}, bf16[2,1,128,2,128]{2,4,0,3,1:T(8,128)(2,1)S(1)}, u32[]{:S(2)}, u32[]{:S(2)}) collective-permute-start(bf16[2,1,128,2,128]{2,4,0,3,1:T(8,128)(2,1)S(1)} %pad_maximum_fusion.4), channel_id=1, source_target_pairs={{0,128},{16,144},{32,160},{48,176},{64,192},{80,208},{96,224},{112... | collective-permute-start | bytes 393224 | tf_op jit(solution)/shard_map/ppermute | solution.py:13
  143.4 11.5 %collective-permute-start.10 = (bf16[2,1,128,2,128]{2,4,0,3,1:T(8,128)(2,1)S(1)}, bf16[2,1,128,2,128]{2,4,0,3,1:T(8,128)(2,1)S(1)}, u32[]{:S(2)}, u32[]{:S(2)}) collective-permute-start(bf16[2,1,128,2,128]{2,4,0,3,1:T(8,128)(2,1)S(1)} %pad_maximum_fusion.5), channel_id=1, source_target_pairs={{0,256},{16,272},{32,288},{48,304},{64,320},{80,336},{96,352},{112... | collective-permute-start | bytes 393224 | tf_op jit(solution)/shard_map/ppermute | solution.py:13
  148.2 14.4 %collective-permute-start.11 = (bf16[2,1,128,2,128]{2,4,0,3,1:T(8,128)(2,1)S(1)}, bf16[2,1,128,2,128]{2,4,0,3,1:T(8,128)(2,1)S(1)}, u32[]{:S(2)}, u32[]{:S(2)}) collective-permute-start(bf16[2,1,128,2,128]{2,4,0,3,1:T(8,128)(2,1)S(1)} %pad_maximum_fusion.6), channel_id=1, source_target_pairs={{0,512},{16,528},{32,544},{48,560},{64,576},{80,592},{96,608},{112... | collective-permute-start | bytes 393224 | tf_op jit(solution)/shard_map/ppermute | solution.py:13
  151.9 10.7 %collective-permute-start.6 = (bf16[2,1,128,2,128]{2,4,0,3,1:T(8,128)(2,1)S(1)}, bf16[2,1,128,2,128]{2,4,0,3,1:T(8,128)(2,1)S(1)}, u32[]{:S(2)}, u32[]{:S(2)}) collective-permute-start(bf16[2,1,128,2,128]{2,4,0,3,1:T(8,128)(2,1)S(1)} %pad_maximum_fusion.1), channel_id=1, source_target_pairs={{0,16},{16,0},{32,48},{48,32},{64,80},{80,64},{96,112},{112,96},{1... | collective-permute-start | bytes 393224 | tf_op jit(solution)/shard_map/ppermute | solution.py:13
  (7 other events, 46.9 us)
Sparse Core Ops, SparseCore 0:
  64.8 21.0 all-gather.1

commit v2 on v1

--- a/solution.py
+++ b/solution.py
@@ -11,29 +11,6 @@
 
 def swapped(shard, axis, distance):
     return lax.ppermute(shard, axis, [(i, i ^ 1 << distance) for i in range(lax.axis_size(axis))])
-
-
-def halving_scatter(partial, axis, levels):
-    rows, cols = partial.shape
-    here = lax.axis_index(axis)
-    block = rows >> levels
-    pieces = partial.reshape((2,) * levels + (2, block // 2, cols))
-    low = [b for b in range(levels) if b < (levels + 1) // 2]
-    high = [b for b in range(levels) if b >= (levels + 1) // 2]
-    first = [b for pair in zip(low, high) for b in pair] + low[len(high):]
-    second = [b for pair in zip(high, low) for b in pair] + low[len(high):]
-    halves = [pieces[..., 0, :, :], pieces[..., 1, :, :]]
-    bits_left = [list(range(levels - 1, -1, -1)), list(range(levels - 1, -1, -1))]
-    for step in range(levels):
-        for h, order in enumerate((first, second)):
-            bit = order[step]
-            at = bits_left[h].index(bit)
-            mine = (here >> bit) & 1
-            keep = lax.dynamic_index_in_dim(halves[h], mine, at, keepdims=False)
-            send = lax.dynamic_index_in_dim(halves[h], 1 - mine, at, keepdims=False)
-            halves[h] = keep + swapped(send, axis, bit)
-            bits_left[h].pop(at)
-    return jnp.concatenate(halves, axis=0)
 
 
 def per_device(query, keys, values, grad_out, w_out, link_flags):
@@ -89,7 +66,9 @@
     partial = lax.dot_general(
         token_rows, token_cols, (((0,), (0,)), ((), ())), preferred_element_type=jnp.float32
     )
-    grad_w = halving_scatter(partial, "seq", levels)
+    n_seq = lax.axis_size("seq")
+    pieces = partial.reshape(n_seq, partial.shape[0] // n_seq, partial.shape[1])
+    grad_w = jnp.sum(lax.all_to_all(pieces.astype(jnp.bfloat16), "seq", 0, 0, tiled=False).astype(jnp.float32), axis=0)
     grad_probs = jnp.einsum(
         "sthc,msuhc->shtmu", grad_heads, value_near, preferred_element_type=jnp.float32
     )

time: 172 us -> 143 us (0.83)
  the two profiles are of different devices: /device:TPU:12 before, /device:TPU:1 now
where the time goes in v2:
time: 143 us; the launch traced here: 140 us
  starting transfers between devices  77.8 us (54%)
  waiting for transfers between devices  26.8 us (19%)
  between operations  14.5 us (10%)
  matrix products  8.58 us (6%)
  other arithmetic  6.74 us (5%)
  local copies, waits for them, and re-layouts  5.64 us (4%)
    ppermute x14, starting transfers between devices, swapped(): lax.ppermute(shard, axis, [(i, i ^ 1 << distance) for i in range(lax.axis...  69.5 us
    ppermute x14, waiting for transfers between devices, swapped(): lax.ppermute(shard, axis, [(i, i ^ 1 << distance) for i in range(lax.axis...  26.8 us
    all_to_all x1, starting transfers between devices, per_device(): lax.all_to_all(pieces.astype(jnp.bfloat16), 'seq', 0, 0, tiled=False)  8.29 us
    unnamed x14, local copies, waits for them, and re-layouts  4.32 us
    another operation x6, other arithmetic, per_device(): jnp.stack([key_terms[level + 1], value_terms[level + 1]])  3.33 us
    dot_general x1, matrix products, per_device(): lax.dot_general(token_rows, token_cols, (((0,), (0,)), ((), ())), preferr...  2.95 us
  transfers between devices with their start and end apart: 16, of which 3 were waited for; matrix products, arithmetic and copies ran while one was open for 13% of the time, Pallas kernels for 0%

profile of v2, /device:TPU:1, one launch (start us, length us, event | category | flops | bytes accessed | tf_op | source)
XLA Modules:
  0.0 140.0 jit_solution(15145316216624418817)
XLA Ops:
  7.2 1.0 copy.23
  8.3 1.0 copy.24
  9.3 11.5 %collective-permute-start.5 = (bf16[2,1,128,256]{2,3,0,1:T(8,128)(2,1)S(1)}, bf16[2,1,128,256]{2,3,0,1:T(8,128)(2,1)S(1)}, u32[]{:S(2)}, u32[]{:S(2)}) collective-permute-start(bf16[2,1,128,256]{2,3,0,1:T(8,128)(2,1)S(1)} %pad_maximum_fusion), channel_id=1, source_target_pairs={{0,512},{16,528},{32,544},{48,560},{64,576},{80,592},{96,608},{112... | collective-permute-start | bytes 393224 | tf_op jit(solution)/shard_map/ppermute | solution.py:13
  20.7 5.8 %collective-permute-start.4 = (bf16[2,1,128,256]{2,3,0,1:T(8,128)(2,1)S(1)}, bf16[2,1,128,256]{2,3,0,1:T(8,128)(2,1)S(1)}, u32[]{:S(2)}, u32[]{:S(2)}) collective-permute-start(bf16[2,1,128,256]{2,3,0,1:T(8,128)(2,1)S(1)} %pad_maximum_fusion), channel_id=1, source_target_pairs={{0,256},{16,272},{32,288},{48,304},{64,320},{80,336},{96,352},{112... | collective-permute-start | bytes 393224 | tf_op jit(solution)/shard_map/ppermute | solution.py:13
  26.5 4.0 %collective-permute-start.3 = (bf16[2,1,128,256]{2,3,0,1:T(8,128)(2,1)S(1)}, bf16[2,1,128,256]{2,3,0,1:T(8,128)(2,1)S(1)}, u32[]{:S(2)}, u32[]{:S(2)}) collective-permute-start(bf16[2,1,128,256]{2,3,0,1:T(8,128)(2,1)S(1)} %pad_maximum_fusion), channel_id=1, source_target_pairs={{0,128},{16,144},{32,160},{48,176},{64,192},{80,208},{96,224},{112... | collective-permute-start | bytes 393224 | tf_op jit(solution)/shard_map/ppermute | solution.py:13
  30.5 4.2 %collective-permute-start.1 = (bf16[2,1,128,256]{2,3,0,1:T(8,128)(2,1)S(1)}, bf16[2,1,128,256]{2,3,0,1:T(8,128)(2,1)S(1)}, u32[]{:S(2)}, u32[]{:S(2)}) collective-permute-start(bf16[2,1,128,256]{2,3,0,1:T(8,128)(2,1)S(1)} %pad_maximum_fusion), channel_id=1, source_target_pairs={{0,32},{16,48},{32,0},{48,16},{64,96},{80,112},{96,64},{112,80},{1... | collective-permute-start | bytes 393224 | tf_op jit(solution)/shard_map/ppermute | solution.py:13
  34.8 3.2 %collective-permute-start = (bf16[2,1,128,256]{2,3,0,1:T(8,128)(2,1)S(1)}, bf16[2,1,128,256]{2,3,0,1:T(8,128)(2,1)S(1)}, u32[]{:S(2)}, u32[]{:S(2)}) collective-permute-start(bf16[2,1,128,256]{2,3,0,1:T(8,128)(2,1)S(1)} %pad_maximum_fusion), channel_id=1, source_target_pairs={{0,16},{16,0},{32,48},{48,32},{64,80},{80,64},{96,112},{112,96},{1... | collective-permute-start | bytes 393224 | tf_op jit(solution)/shard_map/ppermute | solution.py:13
  39.3 2.8 %collective-permute-done = bf16[2,1,128,256]{2,3,0,1:T(8,128)(2,1)S(1)} collective-permute-done((bf16[2,1,128,256]{2,3,0,1:T(8,128)(2,1)S(1)}, bf16[2,1,128,256]{2,3,0,1:T(8,128)(2,1)S(1)}, u32[]{:S(2)}, u32[]{:S(2)}) %collective-permute-start) | collective-permute-done | bytes 131104 | tf_op jit(solution)/shard_map/ppermute | solution.py:13
  42.1 5.1 %collective-permute-start.2 = (bf16[2,1,128,256]{2,3,0,1:T(8,128)(2,1)S(1)}, bf16[2,1,128,256]{2,3,0,1:T(8,128)(2,1)S(1)}, u32[]{:S(2)}, u32[]{:S(2)}) collective-permute-start(bf16[2,1,128,256]{2,3,0,1:T(8,128)(2,1)S(1)} %pad_maximum_fusion), channel_id=1, source_target_pairs={{0,64},{16,80},{32,96},{48,112},{64,0},{80,16},{96,32},{112,48},{1... | collective-permute-start | bytes 393224 | tf_op jit(solution)/shard_map/ppermute | solution.py:13
  47.5 5.7 %collective-permute-start.12 = (bf16[128,4096]{1,0:T(8,128)(2,1)S(1)}, bf16[128,4096]{1,0:T(8,128)(2,1)}, u32[]{:S(2)}, u32[]{:S(2)}) collective-permute-start(bf16[128,4096]{1,0:T(8,128)(2,1)S(1)} %bitcast.85), channel_id=1, source_target_pairs={{0,1},{1,0},{2,3},{3,2},{4,5},{5,4},{6,7},{7,6},{8,9},{9,8},{10,11... | collective-permute-start | bytes 3145736 | tf_op jit(solution)/shard_map/ppermute | solution.py:13
  54.9 4.4 %collective-permute-start.13 = (bf16[128,128]{0,1:T(8,128)(2,1)S(1)}, bf16[128,128]{0,1:T(8,128)(2,1)S(1)}, u32[]{:S(2)}, u32[]{:S(2)}) collective-permute-start(bf16[128,128]{0,1:T(8,128)(2,1)S(1)} %get-tuple-element.27), channel_id=1, source_target_pairs={{0,1},{1,0},{2,3},{3,2},{4,5},{5,4},{6,7},{7,6},{8,9},{9,8},{10,11... | collective-permute-start | bytes 98312 | tf_op jit(solution)/shard_map/ppermute | solution.py:13
  59.3 0.9 collective-permute-done.13
  60.2 2.9 %convolution_convert_fusion = bf16[4096,128]{1,0:T(8,128)(2,1)} fusion(bf16[128,4096]{1,0:T(8,128)(2,1)} %collective-permute-done.12, bf16[128,4096]{1,0:T(8,128)(2,1)S(1)} %bitcast.86, bf16[128,128]{0,1:T(8,128)(2,1)S(1)} %collective-permute-done.13, bf16[128,128]{0,1:T(8,128)(2,1)S(1)} %get-tuple-element.26), kind=kOutput, calls=%fused_computation | convolution fusion | flops 273285120 | bytes 3211264 | tf_op jit(solution)/shard_map/dot_general | solution.py:66
  63.1 8.3 %all-to-all-start = ((bf16[64,64,128]{2,1,0:T(8,128)(2,1)}), bf16[64,64,128]{2,1,0:T(8,128)(2,1)S(1)}, u32[]{:S(2)}, u32[]{:S(2)}) async-start(bf16[64,64,128]{2,1,0:T(8,128)(2,1)} %bitcast.87), calls=%async_computation | async-start | bytes 2097152 | tf_op jit(solution)/shard_map/all_to_all | solution.py:71
  71.5 2.8 %convolution_convert_fusion.1 = bf16[128,256]{1,0:T(8,128)(2,1)S(1)} fusion(bf16[256,4096]{1,0:T(8,128)(2,1)} %all-gather.2.cloned.1.call-done, bf16[1,128,4096]{2,1,0:T(8,128)(2,1)} %param.9), kind=kOutput, calls=%fused_computation.12 | convolution fusion | flops 268468224 | bytes 3211264 | tf_op jit(solution)/shard_map/dot_general | solution.py:50
  74.3 1.3 fusion.39
  76.7 3.8 %collective-permute-start.7 = (bf16[2,1,128,2,128]{2,4,0,3,1:T(8,128)(2,1)S(1)}, bf16[2,1,128,2,128]{2,4,0,3,1:T(8,128)(2,1)S(1)}, u32[]{:S(2)}, u32[]{:S(2)}) collective-permute-start(bf16[2,1,128,2,128]{2,4,0,3,1:T(8,128)(2,1)S(1)} %pad_maximum_fusion.2), channel_id=1, source_target_pairs={{0,32},{16,48},{32,0},{48,16},{64,96},{80,112},{96,64},{112,80},{1... | collective-permute-start | bytes 393224 | tf_op jit(solution)/shard_map/ppermute | solution.py:13
  81.2 5.2 %collective-permute-start.8 = (bf16[2,1,128,2,128]{2,4,0,3,1:T(8,128)(2,1)}, bf16[2,1,128,2,128]{2,4,0,3,1:T(8,128)(2,1)S(1)}, u32[]{:S(2)}, u32[]{:S(2)}) collective-permute-start(bf16[2,1,128,2,128]{2,4,0,3,1:T(8,128)(2,1)} %pad_maximum_fusion.3), channel_id=1, source_target_pairs={{0,64},{16,80},{32,96},{48,112},{64,0},{80,16},{96,32},{112,48},{1... | collective-permute-start | bytes 393224 | tf_op jit(solution)/shard_map/ppermute | solution.py:13
  87.0 3.1 %collective-permute-start.9 = (bf16[2,1,128,2,128]{2,4,0,3,1:T(8,128)(2,1)}, bf16[2,1,128,2,128]{2,4,0,3,1:T(8,128)(2,1)S(1)}, u32[]{:S(2)}, u32[]{:S(2)}) collective-permute-start(bf16[2,1,128,2,128]{2,4,0,3,1:T(8,128)(2,1)} %pad_maximum_fusion.4), channel_id=1, source_target_pairs={{0,128},{16,144},{32,160},{48,176},{64,192},{80,208},{96,224},{112... | collective-permute-start | bytes 393224 | tf_op jit(solution)/shard_map/ppermute | solution.py:13
  90.8 4.1 %collective-permute-start.10 = (bf16[2,1,128,2,128]{2,4,0,3,1:T(8,128)(2,1)}, bf16[2,1,128,2,128]{2,4,0,3,1:T(8,128)(2,1)S(1)}, u32[]{:S(2)}, u32[]{:S(2)}) collective-permute-start(bf16[2,1,128,2,128]{2,4,0,3,1:T(8,128)(2,1)} %pad_maximum_fusion.5), channel_id=1, source_target_pairs={{0,256},{16,272},{32,288},{48,304},{64,320},{80,336},{96,352},{112... | collective-permute-start | bytes 393224 | tf_op jit(solution)/shard_map/ppermute | solution.py:13
  95.5 7.2 %collective-permute-start.11 = (bf16[2,1,128,2,128]{2,4,0,3,1:T(8,128)(2,1)}, bf16[2,1,128,2,128]{2,4,0,3,1:T(8,128)(2,1)}, u32[]{:S(2)}, u32[]{:S(2)}) collective-permute-start(bf16[2,1,128,2,128]{2,4,0,3,1:T(8,128)(2,1)} %pad_maximum_fusion.6), channel_id=1, source_target_pairs={{0,512},{16,528},{32,544},{48,560},{64,576},{80,592},{96,608},{112... | collective-permute-start | bytes 393224 | tf_op jit(solution)/shard_map/ppermute | solution.py:13
  103.4 2.2 %collective-permute-start.6 = (bf16[2,1,128,2,128]{2,4,0,3,1:T(8,128)(2,1)}, bf16[2,1,128,2,128]{2,4,0,3,1:T(8,128)(2,1)}, u32[]{:S(2)}, u32[]{:S(2)}) collective-permute-start(bf16[2,1,128,2,128]{2,4,0,3,1:T(8,128)(2,1)} %pad_maximum_fusion.1), channel_id=1, source_target_pairs={{0,16},{16,0},{32,48},{48,32},{64,80},{80,64},{96,112},{112,96},{1... | collective-permute-start | bytes 393224 | tf_op jit(solution)/shard_map/ppermute | solution.py:13
  106.7 23.1 %collective-permute-done.11 = bf16[2,1,128,2,128]{2,4,0,3,1:T(8,128)(2,1)} collective-permute-done((bf16[2,1,128,2,128]{2,4,0,3,1:T(8,128)(2,1)}, bf16[2,1,128,2,128]{2,4,0,3,1:T(8,128)(2,1)}, u32[]{:S(2)}, u32[]{:S(2)}) %collective-permute-start.11) | collective-permute-done | bytes 131104 | tf_op jit(solution)/shard_map/ppermute | solution.py:13
  129.8 1.1 fusion.17
  (64 shorter events, 11.0 us)
Async XLA Ops:
  7.2 32.0 %copy-start.1 = (bf16[1,128,256]{2,1,0:T(8,128)(2,1)S(1)}, bf16[1,128,256]{2,1,0:T(8,128)(2,1)}, u32[]{:S(2)}) copy-start(bf16[1,128,256]{2,1,0:T(8,128)(2,1)} %param.6) | copy-start | bytes 196612
  7.2 40.3 %copy-start = (bf16[1,128,4096]{2,1,0:T(8,128)(2,1)S(1)}, bf16[1,128,4096]{2,1,0:T(8,128)(2,1)}, u32[]{:S(2)}) copy-start(bf16[1,128,4096]{2,1,0:T(8,128)(2,1)} %param.9) | copy-start | bytes 3145732
  7.2 64.3 %all-gather.2.cloned.1.call-start = ((), (), s32[]{:S(2)}) async-start(), calls=%async_computation.1 | async-start | bytes 3145728 | tf_op jit(solution)/shard_map/all_gather | solution.py:52
  9.3 44.5 %collective-permute-start.5 = (bf16[2,1,128,256]{2,3,0,1:T(8,128)(2,1)S(1)}, bf16[2,1,128,256]{2,3,0,1:T(8,128)(2,1)S(1)}, u32[]{:S(2)}, u32[]{:S(2)}) collective-permute-start(bf16[2,1,128,256]{2,3,0,1:T(8,128)(2,1)S(1)} %pad_maximum_fusion), channel_id=1, source_target_pairs={{0,512},{16,528},{32,544},{48,560},{64,576},{80,592},{96,608},{112... | collective-permute-start | bytes 393224 | tf_op jit(solution)/shard_map/ppermute | solution.py:13
  20.7 33.1 %collective-permute-start.4 = (bf16[2,1,128,256]{2,3,0,1:T(8,128)(2,1)S(1)}, bf16[2,1,128,256]{2,3,0,1:T(8,128)(2,1)S(1)}, u32[]{:S(2)}, u32[]{:S(2)}) collective-permute-start(bf16[2,1,128,256]{2,3,0,1:T(8,128)(2,1)S(1)} %pad_maximum_fusion), channel_id=1, source_target_pairs={{0,256},{16,272},{32,288},{48,304},{64,320},{80,336},{96,352},{112... | collective-permute-start | bytes 393224 | tf_op jit(solution)/shard_map/ppermute | solution.py:13
  26.5 27.0 %collective-permute-start.3 = (bf16[2,1,128,256]{2,3,0,1:T(8,128)(2,1)S(1)}, bf16[2,1,128,256]{2,3,0,1:T(8,128)(2,1)S(1)}, u32[]{:S(2)}, u32[]{:S(2)}) collective-permute-start(bf16[2,1,128,256]{2,3,0,1:T(8,128)(2,1)S(1)} %pad_maximum_fusion), channel_id=1, source_target_pairs={{0,128},{16,144},{32,160},{48,176},{64,192},{80,208},{96,224},{112... | collective-permute-start | bytes 393224 | tf_op jit(solution)/shard_map/ppermute | solution.py:13
  30.5 16.9 %collective-permute-start.1 = (bf16[2,1,128,256]{2,3,0,1:T(8,128)(2,1)S(1)}, bf16[2,1,128,256]{2,3,0,1:T(8,128)(2,1)S(1)}, u32[]{:S(2)}, u32[]{:S(2)}) collective-permute-start(bf16[2,1,128,256]{2,3,0,1:T(8,128)(2,1)S(1)} %pad_maximum_fusion), channel_id=1, source_target_pairs={{0,32},{16,48},{32,0},{48,16},{64,96},{80,112},{96,64},{112,80},{1... | collective-permute-start | bytes 393224 | tf_op jit(solution)/shard_map/ppermute | solution.py:13
  34.8 7.4 %collective-permute-start = (bf16[2,1,128,256]{2,3,0,1:T(8,128)(2,1)S(1)}, bf16[2,1,128,256]{2,3,0,1:T(8,128)(2,1)S(1)}, u32[]{:S(2)}, u32[]{:S(2)}) collective-permute-start(bf16[2,1,128,256]{2,3,0,1:T(8,128)(2,1)S(1)} %pad_maximum_fusion), channel_id=1, source_target_pairs={{0,16},{16,0},{32,48},{48,32},{64,80},{80,64},{96,112},{112,96},{1... | collective-permute-start | bytes 393224 | tf_op jit(solution)/shard_map/ppermute | solution.py:13
  42.1 11.2 %collective-permute-start.2 = (bf16[2,1,128,256]{2,3,0,1:T(8,128)(2,1)S(1)}, bf16[2,1,128,256]{2,3,0,1:T(8,128)(2,1)S(1)}, u32[]{:S(2)}, u32[]{:S(2)}) collective-permute-start(bf16[2,1,128,256]{2,3,0,1:T(8,128)(2,1)S(1)} %pad_maximum_fusion), channel_id=1, source_target_pairs={{0,64},{16,80},{32,96},{48,112},{64,0},{80,16},{96,32},{112,48},{1... | collective-permute-start | bytes 393224 | tf_op jit(solution)/shard_map/ppermute | solution.py:13
  47.5 12.7 %collective-permute-start.12 = (bf16[128,4096]{1,0:T(8,128)(2,1)S(1)}, bf16[128,4096]{1,0:T(8,128)(2,1)}, u32[]{:S(2)}, u32[]{:S(2)}) collective-permute-start(bf16[128,4096]{1,0:T(8,128)(2,1)S(1)} %bitcast.85), channel_id=1, source_target_pairs={{0,1},{1,0},{2,3},{3,2},{4,5},{5,4},{6,7},{7,6},{8,9},{9,8},{10,11... | collective-permute-start | bytes 3145736 | tf_op jit(solution)/shard_map/ppermute | solution.py:13
  54.9 5.2 %collective-permute-start.13 = (bf16[128,128]{0,1:T(8,128)(2,1)S(1)}, bf16[128,128]{0,1:T(8,128)(2,1)S(1)}, u32[]{:S(2)}, u32[]{:S(2)}) collective-permute-start(bf16[128,128]{0,1:T(8,128)(2,1)S(1)} %get-tuple-element.27), channel_id=1, source_target_pairs={{0,1},{1,0},{2,3},{3,2},{4,5},{5,4},{6,7},{7,6},{8,9},{9,8},{10,11... | collective-permute-start | bytes 98312 | tf_op jit(solution)/shard_map/ppermute | solution.py:13
  63.1 69.3 %all-to-all-start = ((bf16[64,64,128]{2,1,0:T(8,128)(2,1)}), bf16[64,64,128]{2,1,0:T(8,128)(2,1)S(1)}, u32[]{:S(2)}, u32[]{:S(2)}) async-start(bf16[64,64,128]{2,1,0:T(8,128)(2,1)} %bitcast.87), calls=%async_computation | async-start | bytes 2097152 | tf_op jit(solution)/shard_map/all_to_all | solution.py:71
  76.7 26.7 %collective-permute-start.7 = (bf16[2,1,128,2,128]{2,4,0,3,1:T(8,128)(2,1)S(1)}, bf16[2,1,128,2,128]{2,4,0,3,1:T(8,128)(2,1)S(1)}, u32[]{:S(2)}, u32[]{:S(2)}) collective-permute-start(bf16[2,1,128,2,128]{2,4,0,3,1:T(8,128)(2,1)S(1)} %pad_maximum_fusion.2), channel_id=1, source_target_pairs={{0,32},{16,48},{32,0},{48,16},{64,96},{80,112},{96,64},{112,80},{1... | collective-permute-start | bytes 393224 | tf_op jit(solution)/shard_map/ppermute | solution.py:13
  81.2 25.5 %collective-permute-start.8 = (bf16[2,1,128,2,128]{2,4,0,3,1:T(8,128)(2,1)}, bf16[2,1,128,2,128]{2,4,0,3,1:T(8,128)(2,1)S(1)}, u32[]{:S(2)}, u32[]{:S(2)}) collective-permute-start(bf16[2,1,128,2,128]{2,4,0,3,1:T(8,128)(2,1)} %pad_maximum_fusion.3), channel_id=1, source_target_pairs={{0,64},{16,80},{32,96},{48,112},{64,0},{80,16},{96,32},{112,48},{1... | collective-permute-start | bytes 393224 | tf_op jit(solution)/shard_map/ppermute | solution.py:13
  87.0 19.6 %collective-permute-start.9 = (bf16[2,1,128,2,128]{2,4,0,3,1:T(8,128)(2,1)}, bf16[2,1,128,2,128]{2,4,0,3,1:T(8,128)(2,1)S(1)}, u32[]{:S(2)}, u32[]{:S(2)}) collective-permute-start(bf16[2,1,128,2,128]{2,4,0,3,1:T(8,128)(2,1)} %pad_maximum_fusion.4), channel_id=1, source_target_pairs={{0,128},{16,144},{32,160},{48,176},{64,192},{80,208},{96,224},{112... | collective-permute-start | bytes 393224 | tf_op jit(solution)/shard_map/ppermute | solution.py:13
  90.8 15.9 %collective-permute-start.10 = (bf16[2,1,128,2,128]{2,4,0,3,1:T(8,128)(2,1)}, bf16[2,1,128,2,128]{2,4,0,3,1:T(8,128)(2,1)S(1)}, u32[]{:S(2)}, u32[]{:S(2)}) collective-permute-start(bf16[2,1,128,2,128]{2,4,0,3,1:T(8,128)(2,1)} %pad_maximum_fusion.5), channel_id=1, source_target_pairs={{0,256},{16,272},{32,288},{48,304},{64,320},{80,336},{96,352},{112... | collective-permute-start | bytes 393224 | tf_op jit(solution)/shard_map/ppermute | solution.py:13
  95.5 34.3 %collective-permute-start.11 = (bf16[2,1,128,2,128]{2,4,0,3,1:T(8,128)(2,1)}, bf16[2,1,128,2,128]{2,4,0,3,1:T(8,128)(2,1)}, u32[]{:S(2)}, u32[]{:S(2)}) collective-permute-start(bf16[2,1,128,2,128]{2,4,0,3,1:T(8,128)(2,1)} %pad_maximum_fusion.6), channel_id=1, source_target_pairs={{0,512},{16,528},{32,544},{48,560},{64,576},{80,592},{96,608},{112... | collective-permute-start | bytes 393224 | tf_op jit(solution)/shard_map/ppermute | solution.py:13
  103.4 26.4 %collective-permute-start.6 = (bf16[2,1,128,2,128]{2,4,0,3,1:T(8,128)(2,1)}, bf16[2,1,128,2,128]{2,4,0,3,1:T(8,128)(2,1)}, u32[]{:S(2)}, u32[]{:S(2)}) collective-permute-start(bf16[2,1,128,2,128]{2,4,0,3,1:T(8,128)(2,1)} %pad_maximum_fusion.1), channel_id=1, source_target_pairs={{0,16},{16,0},{32,48},{48,32},{64,80},{80,64},{96,112},{112,96},{1... | collective-permute-start | bytes 393224 | tf_op jit(solution)/shard_map/ppermute | solution.py:13
Sparse Core Ops, SparseCore 0:
  38.1 25.8 all-gather.1

commit v3 on v2

--- a/solution.py
+++ b/solution.py
@@ -5,23 +5,32 @@
 from jax import lax
 from jax.sharding import PartitionSpec as P
 
+
 D = 4096
 HD = 128
 
 
-def swapped(shard, axis, distance):
-    return lax.ppermute(shard, axis, [(i, i ^ 1 << distance) for i in range(lax.axis_size(axis))])
+SEQ = ("seq_hi", "seq_lo")
 
 
-def per_device(query, keys, values, grad_out, w_out, link_flags):
+def size_of(axis):
+    names = axis if isinstance(axis, tuple) else (axis,)
+    return math.prod(lax.axis_size(name) for name in names)
+
+
+def swapped(shard, axis, distance):
+    return lax.ppermute(shard, axis, [(i, i ^ 1 << distance) for i in range(size_of(axis))])
+
+
+def per_device_body(query, keys, values, grad_out, w_out, link_flags):
     local_seqs, block_len, local_width = query.shape
     local_heads = local_width // HD
-    levels = lax.axis_size("seq").bit_length() - 1
+    levels = size_of(SEQ).bit_length() - 1
     score_scale = 1.0 / math.sqrt(HD)
     key_value = jnp.stack([keys, values])
     collected = [key_value]
     for level in range(levels):
-        collected.append(swapped(key_value, "seq", level))
+        collected.append(swapped(key_value, SEQ, level))
     slots = levels + 1
     near_all = jnp.stack(collected).reshape(slots, 2, local_seqs, block_len, local_heads, HD)
     key_near = near_all[:, 0]
@@ -66,9 +75,13 @@
     partial = lax.dot_general(
         token_rows, token_cols, (((0,), (0,)), ((), ())), preferred_element_type=jnp.float32
     )
-    n_seq = lax.axis_size("seq")
-    pieces = partial.reshape(n_seq, partial.shape[0] // n_seq, partial.shape[1])
-    grad_w = jnp.sum(lax.all_to_all(pieces.astype(jnp.bfloat16), "seq", 0, 0, tiled=False).astype(jnp.float32), axis=0)
+    n_hi = lax.axis_size("seq_hi")
+    n_lo = lax.axis_size("seq_lo")
+    pieces = partial.reshape(n_hi, n_lo, partial.shape[0] // (n_hi * n_lo), partial.shape[1])
+    inner = lax.all_to_all(pieces.astype(jnp.bfloat16), "seq_lo", 1, 1, tiled=False)
+    inner = jnp.sum(inner.astype(jnp.float32), axis=1)
+    outer = lax.all_to_all(inner.astype(jnp.bfloat16), "seq_hi", 0, 0, tiled=False)
+    grad_w = jnp.sum(outer.astype(jnp.float32), axis=0)
     grad_probs = jnp.einsum(
         "sthc,msuhc->shtmu", grad_heads, value_near, preferred_element_type=jnp.float32
     )
@@ -87,7 +100,7 @@
     grad_value = value_terms[0]
     for level in range(levels):
         outgoing = jnp.stack([key_terms[level + 1], value_terms[level + 1]]).astype(jnp.bfloat16)
-        returned = swapped(outgoing, "seq", level)
+        returned = swapped(outgoing, SEQ, level)
         grad_key = grad_key + returned[0].astype(jnp.float32)
         grad_value = grad_value + returned[1].astype(jnp.float32)
     shape_out = (local_seqs, block_len, local_width)
@@ -100,20 +113,24 @@
 
 
 def solution(mesh):
+    n_seq = mesh.shape["seq"]
+    n_lo = min(8, n_seq)
+    devices = mesh.devices.reshape(n_seq // n_lo, n_lo, *mesh.devices.shape[1:])
+    mesh = jax.sharding.Mesh(devices, SEQ + mesh.axis_names[1:])
     in_specs = (
-        P("fsdp", "seq", "head"),
-        P("fsdp", "seq", "head"),
-        P("fsdp", "seq", "head"),
-        P("fsdp", "seq", None),
+        P("fsdp", SEQ, "head"),
+        P("fsdp", SEQ, "head"),
+        P("fsdp", SEQ, "head"),
+        P("fsdp", SEQ, None),
         P("head", "fsdp"),
-        P("seq", None),
+        P(SEQ, None),
     )
     out_specs = (
-        P("fsdp", "seq", "head"),
-        P("fsdp", "seq", "head"),
-        P("fsdp", "seq", "head"),
-        P("seq", ("head", "fsdp")),
+        P("fsdp", SEQ, "head"),
+        P("fsdp", SEQ, "head"),
+        P("fsdp", SEQ, "head"),
+        P(SEQ, ("head", "fsdp")),
     )
     return jax.shard_map(
-        per_device, mesh=mesh, in_specs=in_specs, out_specs=out_specs, check_vma=False
+        per_device_body, mesh=mesh, in_specs=in_specs, out_specs=out_specs, check_vma=False
     )

time: 143 us -> 121 us (0.85); the launches traced: 140 us -> 120 us
  waiting for transfers between devices: 26.8 us -> 9.95 us
  starting transfers between devices: 77.8 us -> 72.4 us
  local copies, waits for them, and re-layouts: 5.64 us -> 7.54 us
  other arithmetic: 6.74 us -> 8.19 us
    ppermute x14, waiting for transfers between devices: 26.8 us -> 5.05 us  [swapped(): lax.ppermute(shard, axis, [(i, i ^ 1 << distance) for i in range(size_of(...]
    ppermute x14, starting transfers between devices: 69.5 us -> 65.4 us  [swapped(): lax.ppermute(shard, axis, [(i, i ^ 1 << distance) for i in range(size_of(...]
    all_gather x1, waiting for transfers between devices: 0.02 us -> 2.48 us  [per_device_body(): lax.all_gather(w_out, 'fsdp', axis=1, tiled=True)]
    all_to_all x1 -> x2, waiting for transfers between devices: 0.01 us -> 2.41 us  [the longest x1 2.4 us: per_device_body(): lax.all_to_all(inner.astype(jnp.bfloat16), 'seq_hi', 0, 0, tiled=False)]
    all_to_all x1 -> x2, starting transfers between devices: 8.29 us -> 6.93 us  [the longest x1 3.56 us: per_device_body(): lax.all_to_all(pieces.astype(jnp.bfloat16), 'seq_lo', 1, 1, tiled=False)]
    unnamed x14 -> x12, local copies, waits for them, and re-layouts: 4.32 us -> 4.31 us
  transfers between devices with their start and end apart: 16 -> 17, of which waited for: 3 -> 5; matrix products, arithmetic and copies ran while one was open for 13% -> 17% of each run, Pallas kernels for 0% -> 0%
where the time goes in v3:
time: 121 us; the launch traced here: 120 us
  starting transfers between devices  72.4 us (60%)
  between operations  14.4 us (12%)
  waiting for transfers between devices  9.95 us (8%)
  other arithmetic  8.19 us (7%)
  matrix products  7.61 us (6%)
  local copies, waits for them, and re-layouts  7.54 us (6%)
    ppermute x14, starting transfers between devices, swapped(): lax.ppermute(shard, axis, [(i, i ^ 1 << distance) for i in range(size_of(...  65.4 us
    ppermute x14, waiting for transfers between devices, swapped(): lax.ppermute(shard, axis, [(i, i ^ 1 << distance) for i in range(size_of(...  5.05 us
    unnamed x12, local copies, waits for them, and re-layouts  4.31 us
    another operation x6, other arithmetic, per_device_body(): jnp.stack([key_terms[level + 1], value_terms[level + 1]])  3.97 us
    all_to_all x1, starting transfers between devices, per_device_body(): lax.all_to_all(pieces.astype(jnp.bfloat16), 'seq_lo', 1, 1, tiled=False)  3.56 us
    all_to_all x1, starting transfers between devices, per_device_body(): lax.all_to_all(inner.astype(jnp.bfloat16), 'seq_hi', 0, 0, tiled=False)  3.37 us
    dot_general x1, matrix products, per_device_body(): lax.dot_general(columns, lax.all_gather(w_out, 'fsdp', axis=1, tiled=True...  2.75 us
    all_gather x1, waiting for transfers between devices, per_device_body(): lax.all_gather(w_out, 'fsdp', axis=1, tiled=True)  2.48 us
  transfers between devices with their start and end apart: 17, of which 5 were waited for; matrix products, arithmetic and copies ran while one was open for 17% of the time, Pallas kernels for 0%

profile of v3, /device:TPU:1, one launch (start us, length us, event | category | flops | bytes accessed | tf_op | source)
XLA Modules:
  0.0 120.1 jit_solution(4460279311223597705)
XLA Ops:
  9.2 11.5 %collective-permute-start.5 = (bf16[2,1,128,256]{2,3,0,1:T(8,128)(2,1)S(1)}, bf16[2,1,128,256]{2,3,0,1:T(8,128)(2,1)S(1)}, u32[]{:S(2)}, u32[]{:S(2)}) collective-permute-start(bf16[2,1,128,256]{2,3,0,1:T(8,128)(2,1)S(1)} %pad_maximum_fusion), channel_id=1, source_target_pairs={{0,512},{16,528},{32,544},{48,560},{64,576},{80,592},{96,608},{112... | collective-permute-start | bytes 393224 | tf_op jit(solution)/shard_map/ppermute | solution.py:22
  20.7 5.8 %collective-permute-start.4 = (bf16[2,1,128,256]{2,3,0,1:T(8,128)(2,1)S(1)}, bf16[2,1,128,256]{2,3,0,1:T(8,128)(2,1)S(1)}, u32[]{:S(2)}, u32[]{:S(2)}) collective-permute-start(bf16[2,1,128,256]{2,3,0,1:T(8,128)(2,1)S(1)} %pad_maximum_fusion), channel_id=1, source_target_pairs={{0,256},{16,272},{32,288},{48,304},{64,320},{80,336},{96,352},{112... | collective-permute-start | bytes 393224 | tf_op jit(solution)/shard_map/ppermute | solution.py:22
  26.5 4.0 %collective-permute-start.3 = (bf16[2,1,128,256]{2,3,0,1:T(8,128)(2,1)S(1)}, bf16[2,1,128,256]{2,3,0,1:T(8,128)(2,1)S(1)}, u32[]{:S(2)}, u32[]{:S(2)}) collective-permute-start(bf16[2,1,128,256]{2,3,0,1:T(8,128)(2,1)S(1)} %pad_maximum_fusion), channel_id=1, source_target_pairs={{0,128},{16,144},{32,160},{48,176},{64,192},{80,208},{96,224},{112... | collective-permute-start | bytes 393224 | tf_op jit(solution)/shard_map/ppermute | solution.py:22
  30.5 7.5 %collective-permute-start.2 = (bf16[2,1,128,256]{2,3,0,1:T(8,128)(2,1)S(1)}, bf16[2,1,128,256]{2,3,0,1:T(8,128)(2,1)S(1)}, u32[]{:S(2)}, u32[]{:S(2)}) collective-permute-start(bf16[2,1,128,256]{2,3,0,1:T(8,128)(2,1)S(1)} %pad_maximum_fusion), channel_id=1, source_target_pairs={{0,64},{16,80},{32,96},{48,112},{64,0},{80,16},{96,32},{112,48},{1... | collective-permute-start | bytes 393224 | tf_op jit(solution)/shard_map/ppermute | solution.py:22
  38.0 2.4 %collective-permute-start.1 = (bf16[2,1,128,256]{2,3,0,1:T(8,128)(2,1)S(1)}, bf16[2,1,128,256]{2,3,0,1:T(8,128)(2,1)S(1)}, u32[]{:S(2)}, u32[]{:S(2)}) collective-permute-start(bf16[2,1,128,256]{2,3,0,1:T(8,128)(2,1)S(1)} %pad_maximum_fusion), channel_id=1, source_target_pairs={{0,32},{16,48},{32,0},{48,16},{64,96},{80,112},{96,64},{112,80},{1... | collective-permute-start | bytes 393224 | tf_op jit(solution)/shard_map/ppermute | solution.py:22
  41.2 2.3 %collective-permute-start = (bf16[2,1,128,256]{2,3,0,1:T(8,128)(2,1)S(1)}, bf16[2,1,128,256]{2,3,0,1:T(8,128)(2,1)S(1)}, u32[]{:S(2)}, u32[]{:S(2)}) collective-permute-start(bf16[2,1,128,256]{2,3,0,1:T(8,128)(2,1)S(1)} %pad_maximum_fusion), channel_id=1, source_target_pairs={{0,16},{16,0},{32,48},{48,32},{64,80},{80,64},{96,112},{112,96},{1... | collective-permute-start | bytes 393224 | tf_op jit(solution)/shard_map/ppermute | solution.py:22
  45.1 4.3 %collective-permute-start.12 = (bf16[128,4096]{1,0:T(8,128)(2,1)S(1)}, bf16[128,4096]{1,0:T(8,128)(2,1)}, u32[]{:S(2)}, u32[]{:S(2)}) collective-permute-start(bf16[128,4096]{1,0:T(8,128)(2,1)S(1)} %bitcast.85), channel_id=1, source_target_pairs={{0,1},{1,0},{2,3},{3,2},{4,5},{5,4},{6,7},{7,6},{8,9},{9,8},{10,11... | collective-permute-start | bytes 3145736 | tf_op jit(solution)/shard_map/ppermute | solution.py:22
  49.8 1.2 %collective-permute-done.1 = bf16[2,1,128,256]{2,3,0,1:T(8,128)(2,1)S(1)} collective-permute-done((bf16[2,1,128,256]{2,3,0,1:T(8,128)(2,1)S(1)}, bf16[2,1,128,256]{2,3,0,1:T(8,128)(2,1)S(1)}, u32[]{:S(2)}, u32[]{:S(2)}) %collective-permute-start.1) | collective-permute-done | bytes 131104 | tf_op jit(solution)/shard_map/ppermute | solution.py:22
  52.3 3.3 %collective-permute-start.13 = (bf16[128,128]{0,1:T(8,128)(2,1)S(1)}, bf16[128,128]{0,1:T(8,128)(2,1)S(1)}, u32[]{:S(2)}, u32[]{:S(2)}) collective-permute-start(bf16[128,128]{0,1:T(8,128)(2,1)S(1)} %get-tuple-element.35), channel_id=1, source_target_pairs={{0,1},{1,0},{2,3},{3,2},{4,5},{5,4},{6,7},{7,6},{8,9},{9,8},{10,11... | collective-permute-start | bytes 98312 | tf_op jit(solution)/shard_map/ppermute | solution.py:22
  56.5 2.0 %convolution_convert_fusion = bf16[4096,128]{1,0:T(8,128)(2,1)S(1)} fusion(bf16[128,4096]{1,0:T(8,128)(2,1)} %collective-permute-done.12, bf16[128,4096]{1,0:T(8,128)(2,1)S(1)} %bitcast.86, bf16[128,128]{0,1:T(8,128)(2,1)S(1)} %collective-permute-done.13, bf16[128,128]{0,1:T(8,128)(2,1)S(1)} %get-tuple-element.34), kind=kOutput, calls=%fused_computation | convolution fusion | flops 273285120 | bytes 3211264 | tf_op jit(solution)/shard_map/dot_general | solution.py:75
  59.6 3.6 %all-to-all-start = ((bf16[8,8,64,128]{3,2,0,1:T(8,128)(2,1)}), bf16[8,8,64,128]{3,2,0,1:T(8,128)(2,1)S(1)}, u32[]{:S(2)}, u32[]{:S(2)}) async-start(bf16[8,8,64,128]{3,2,0,1:T(8,128)(2,1)} %copy.96), calls=%async_computation | async-start | bytes 2097152 | tf_op jit(solution)/shard_map/all_to_all | solution.py:81
  63.1 2.5 %all-gather.2.cloned.1.call-done = bf16[256,4096]{1,0:T(8,128)(2,1)} async-done(((bf16[256,2048]{1,0:T(8,128)(2,1)}), bf16[256,4096]{1,0:T(8,128)(2,1)}) %all-gather.2.cloned.1.call-update) | async-done | bytes 2097168 | tf_op jit(solution)/shard_map/all_gather | solution.py:61
  65.6 2.8 %convolution_convert_fusion.1 = bf16[128,256]{1,0:T(8,128)(2,1)S(1)} fusion(bf16[256,4096]{1,0:T(8,128)(2,1)} %all-gather.2.cloned.1.call-done, bf16[1,128,4096]{2,1,0:T(8,128)(2,1)} %param.9), kind=kOutput, calls=%fused_computation.11 | convolution fusion | flops 268468224 | bytes 3211264 | tf_op jit(solution)/shard_map/dot_general | solution.py:59
  68.7 1.3 %fusion.39 = (bf16[7,1,128,2,128]{2,4,0,3,1:T(8,128)(2,1)S(1)}, f32[7,1,128,2,128]{2,4,0,3,1:T(8,128)}) fusion(f32[2,128]{1,0:T(2,128)S(1)} %fusion.8, f32[2,128,7,128]{1,3,2,0:T(8,128)S(1)} %get-tuple-element.37, f32[2,128]{1,0:T(2,128)S(1)} %get-tuple-element.36, bf16[128,2,128,1]{2,1,0,3:T(2,128)(2,1)S(1)} %bitcast.102), kind=kOutput, calls=%fused_computation.72 | convolution fusion | flops 59637760 | bytes 2361344 | tf_op jit(solution)/shard_map/shtmu,sthc->msuhc/dot_general | solution.py:96
  71.4 1.9 %collective-permute-start.7 = (bf16[2,1,128,2,128]{2,4,0,3,1:T(8,128)(2,1)}, bf16[2,1,128,2,128]{2,4,0,3,1:T(8,128)(2,1)S(1)}, u32[]{:S(2)}, u32[]{:S(2)}) collective-permute-start(bf16[2,1,128,2,128]{2,4,0,3,1:T(8,128)(2,1)} %pad_maximum_fusion.2), channel_id=1, source_target_pairs={{0,32},{16,48},{32,0},{48,16},{64,96},{80,112},{96,64},{112,80},{1... | collective-permute-start | bytes 393224 | tf_op jit(solution)/shard_map/ppermute | solution.py:22
  74.0 5.0 %collective-permute-start.8 = (bf16[2,1,128,2,128]{2,4,0,3,1:T(8,128)(2,1)}, bf16[2,1,128,2,128]{2,4,0,3,1:T(8,128)(2,1)}, u32[]{:S(2)}, u32[]{:S(2)}) collective-permute-start(bf16[2,1,128,2,128]{2,4,0,3,1:T(8,128)(2,1)} %pad_maximum_fusion.3), channel_id=1, source_target_pairs={{0,64},{16,80},{32,96},{48,112},{64,0},{80,16},{96,32},{112,48},{1... | collective-permute-start | bytes 393224 | tf_op jit(solution)/shard_map/ppermute | solution.py:22
  79.7 3.2 %collective-permute-start.9 = (bf16[2,1,128,2,128]{2,4,0,3,1:T(8,128)(2,1)}, bf16[2,1,128,2,128]{2,4,0,3,1:T(8,128)(2,1)}, u32[]{:S(2)}, u32[]{:S(2)}) collective-permute-start(bf16[2,1,128,2,128]{2,4,0,3,1:T(8,128)(2,1)} %pad_maximum_fusion.4), channel_id=1, source_target_pairs={{0,128},{16,144},{32,160},{48,176},{64,192},{80,208},{96,224},{112... | collective-permute-start | bytes 393224 | tf_op jit(solution)/shard_map/ppermute | solution.py:22
  83.6 4.3 %collective-permute-start.10 = (bf16[2,1,128,2,128]{2,4,0,3,1:T(8,128)(2,1)}, bf16[2,1,128,2,128]{2,4,0,3,1:T(8,128)(2,1)}, u32[]{:S(2)}, u32[]{:S(2)}) collective-permute-start(bf16[2,1,128,2,128]{2,4,0,3,1:T(8,128)(2,1)} %pad_maximum_fusion.5), channel_id=1, source_target_pairs={{0,256},{16,272},{32,288},{48,304},{64,320},{80,336},{96,352},{112... | collective-permute-start | bytes 393224 | tf_op jit(solution)/shard_map/ppermute | solution.py:22
  88.6 7.7 %collective-permute-start.11 = (bf16[2,1,128,2,128]{2,4,0,3,1:T(8,128)(2,1)}, bf16[2,1,128,2,128]{2,4,0,3,1:T(8,128)(2,1)}, u32[]{:S(2)}, u32[]{:S(2)}) collective-permute-start(bf16[2,1,128,2,128]{2,4,0,3,1:T(8,128)(2,1)} %pad_maximum_fusion.6), channel_id=1, source_target_pairs={{0,512},{16,528},{32,544},{48,560},{64,576},{80,592},{96,608},{112... | collective-permute-start | bytes 393224 | tf_op jit(solution)/shard_map/ppermute | solution.py:22
  97.8 3.4 %all-to-all-start.1 = ((bf16[8,64,128]{2,1,0:T(8,128)(2,1)}), bf16[8,64,128]{2,1,0:T(8,128)(2,1)S(1)}, u32[]{:S(2)}, u32[]{:S(2)}) async-start(bf16[8,64,128]{2,1,0:T(8,128)(2,1)} %reduce_sum.41), calls=%async_computation.1 | async-start | bytes 262144 | tf_op jit(solution)/shard_map/all_to_all | solution.py:83
  101.2 2.2 %collective-permute-start.6 = (bf16[2,1,128,2,128]{2,4,0,3,1:T(8,128)(2,1)}, bf16[2,1,128,2,128]{2,4,0,3,1:T(8,128)(2,1)S(1)}, u32[]{:S(2)}, u32[]{:S(2)}) collective-permute-start(bf16[2,1,128,2,128]{2,4,0,3,1:T(8,128)(2,1)} %pad_maximum_fusion.1), channel_id=1, source_target_pairs={{0,16},{16,0},{32,48},{48,32},{64,80},{80,64},{96,112},{112,96},{1... | collective-permute-start | bytes 393224 | tf_op jit(solution)/shard_map/ppermute | solution.py:22
  104.5 3.0 %collective-permute-done.6 = bf16[2,1,128,2,128]{2,4,0,3,1:T(8,128)(2,1)S(1)} collective-permute-done((bf16[2,1,128,2,128]{2,4,0,3,1:T(8,128)(2,1)}, bf16[2,1,128,2,128]{2,4,0,3,1:T(8,128)(2,1)S(1)}, u32[]{:S(2)}, u32[]{:S(2)}) %collective-permute-start.6) | collective-permute-done | bytes 131104 | tf_op jit(solution)/shard_map/ppermute | solution.py:22
  107.5 1.2 %fusion.17 = (bf16[1,1,128,2,128]{2,4,0,3,1:T(8,128)(2,1)S(1)}, bf16[1,1,128,2,128]{2,4,0,3,1:T(8,128)(2,1)S(1)}) fusion(f32[7,1,128,2,128]{2,4,0,3,1:T(8,128)} %get-tuple-element.39, bf16[2,1,128,2,128]{2,4,0,3,1:T(8,128)(2,1)} %collective-permute-done.11, bf16[2,1,128,2,128]{2,4,0,3,1:T(8,128)(2,1)} %collective-permute-done.10, ...), kind=kLoop, calls=%fused_computation.31 | loop fusion | flops 851968 | bytes 1179648 | tf_op jit(solution)/shard_map/convert_element_type | solution.py:110
  110.3 2.4 %all-to-all-done.1 = bf16[8,64,128]{2,1,0:T(8,128)(2,1)S(1)} async-done(((bf16[8,64,128]{2,1,0:T(8,128)(2,1)}), bf16[8,64,128]{2,1,0:T(8,128)(2,1)S(1)}, u32[]{:S(2)}, u32[]{:S(2)}) %all-to-all-start.1) | async-done | bytes 131104 | tf_op jit(solution)/shard_map/all_to_all | solution.py:83
  (66 shorter events, 17.0 us)
Async XLA Ops:
  7.2 37.9 %copy-start = (bf16[1,128,4096]{2,1,0:T(8,128)(2,1)S(1)}, bf16[1,128,4096]{2,1,0:T(8,128)(2,1)}, u32[]{:S(2)}) copy-start(bf16[1,128,4096]{2,1,0:T(8,128)(2,1)} %param.9) | copy-start | bytes 3145732
  7.2 58.4 %all-gather.2.cloned.1.call-start = ((), (), s32[]{:S(2)}) async-start(), calls=%async_computation.2 | async-start | bytes 3145728 | tf_op jit(solution)/shard_map/all_gather | solution.py:61
  9.2 32.0 %collective-permute-start.5 = (bf16[2,1,128,256]{2,3,0,1:T(8,128)(2,1)S(1)}, bf16[2,1,128,256]{2,3,0,1:T(8,128)(2,1)S(1)}, u32[]{:S(2)}, u32[]{:S(2)}) collective-permute-start(bf16[2,1,128,256]{2,3,0,1:T(8,128)(2,1)S(1)} %pad_maximum_fusion), channel_id=1, source_target_pairs={{0,512},{16,528},{32,544},{48,560},{64,576},{80,592},{96,608},{112... | collective-permute-start | bytes 393224 | tf_op jit(solution)/shard_map/ppermute | solution.py:22
  20.7 24.4 %collective-permute-start.4 = (bf16[2,1,128,256]{2,3,0,1:T(8,128)(2,1)S(1)}, bf16[2,1,128,256]{2,3,0,1:T(8,128)(2,1)S(1)}, u32[]{:S(2)}, u32[]{:S(2)}) collective-permute-start(bf16[2,1,128,256]{2,3,0,1:T(8,128)(2,1)S(1)} %pad_maximum_fusion), channel_id=1, source_target_pairs={{0,256},{16,272},{32,288},{48,304},{64,320},{80,336},{96,352},{112... | collective-permute-start | bytes 393224 | tf_op jit(solution)/shard_map/ppermute | solution.py:22
  26.5 23.0 %collective-permute-start.3 = (bf16[2,1,128,256]{2,3,0,1:T(8,128)(2,1)S(1)}, bf16[2,1,128,256]{2,3,0,1:T(8,128)(2,1)S(1)}, u32[]{:S(2)}, u32[]{:S(2)}) collective-permute-start(bf16[2,1,128,256]{2,3,0,1:T(8,128)(2,1)S(1)} %pad_maximum_fusion), channel_id=1, source_target_pairs={{0,128},{16,144},{32,160},{48,176},{64,192},{80,208},{96,224},{112... | collective-permute-start | bytes 393224 | tf_op jit(solution)/shard_map/ppermute | solution.py:22
  30.5 19.1 %collective-permute-start.2 = (bf16[2,1,128,256]{2,3,0,1:T(8,128)(2,1)S(1)}, bf16[2,1,128,256]{2,3,0,1:T(8,128)(2,1)S(1)}, u32[]{:S(2)}, u32[]{:S(2)}) collective-permute-start(bf16[2,1,128,256]{2,3,0,1:T(8,128)(2,1)S(1)} %pad_maximum_fusion), channel_id=1, source_target_pairs={{0,64},{16,80},{32,96},{48,112},{64,0},{80,16},{96,32},{112,48},{1... | collective-permute-start | bytes 393224 | tf_op jit(solution)/shard_map/ppermute | solution.py:22
  38.0 13.0 %collective-permute-start.1 = (bf16[2,1,128,256]{2,3,0,1:T(8,128)(2,1)S(1)}, bf16[2,1,128,256]{2,3,0,1:T(8,128)(2,1)S(1)}, u32[]{:S(2)}, u32[]{:S(2)}) collective-permute-start(bf16[2,1,128,256]{2,3,0,1:T(8,128)(2,1)S(1)} %pad_maximum_fusion), channel_id=1, source_target_pairs={{0,32},{16,48},{32,0},{48,16},{64,96},{80,112},{96,64},{112,80},{1... | collective-permute-start | bytes 393224 | tf_op jit(solution)/shard_map/ppermute | solution.py:22
  41.2 9.9 %collective-permute-start = (bf16[2,1,128,256]{2,3,0,1:T(8,128)(2,1)S(1)}, bf16[2,1,128,256]{2,3,0,1:T(8,128)(2,1)S(1)}, u32[]{:S(2)}, u32[]{:S(2)}) collective-permute-start(bf16[2,1,128,256]{2,3,0,1:T(8,128)(2,1)S(1)} %pad_maximum_fusion), channel_id=1, source_target_pairs={{0,16},{16,0},{32,48},{48,32},{64,80},{80,64},{96,112},{112,96},{1... | collective-permute-start | bytes 393224 | tf_op jit(solution)/shard_map/ppermute | solution.py:22
  45.1 11.4 %collective-permute-start.12 = (bf16[128,4096]{1,0:T(8,128)(2,1)S(1)}, bf16[128,4096]{1,0:T(8,128)(2,1)}, u32[]{:S(2)}, u32[]{:S(2)}) collective-permute-start(bf16[128,4096]{1,0:T(8,128)(2,1)S(1)} %bitcast.85), channel_id=1, source_target_pairs={{0,1},{1,0},{2,3},{3,2},{4,5},{5,4},{6,7},{7,6},{8,9},{9,8},{10,11... | collective-permute-start | bytes 3145736 | tf_op jit(solution)/shard_map/ppermute | solution.py:22
  52.3 4.2 %collective-permute-start.13 = (bf16[128,128]{0,1:T(8,128)(2,1)S(1)}, bf16[128,128]{0,1:T(8,128)(2,1)S(1)}, u32[]{:S(2)}, u32[]{:S(2)}) collective-permute-start(bf16[128,128]{0,1:T(8,128)(2,1)S(1)} %get-tuple-element.35), channel_id=1, source_target_pairs={{0,1},{1,0},{2,3},{3,2},{4,5},{5,4},{6,7},{7,6},{8,9},{9,8},{10,11... | collective-permute-start | bytes 98312 | tf_op jit(solution)/shard_map/ppermute | solution.py:22
  59.6 37.4 %all-to-all-start = ((bf16[8,8,64,128]{3,2,0,1:T(8,128)(2,1)}), bf16[8,8,64,128]{3,2,0,1:T(8,128)(2,1)S(1)}, u32[]{:S(2)}, u32[]{:S(2)}) async-start(bf16[8,8,64,128]{3,2,0,1:T(8,128)(2,1)} %copy.96), calls=%async_computation | async-start | bytes 2097152 | tf_op jit(solution)/shard_map/all_to_all | solution.py:81
  71.4 29.8 %collective-permute-start.7 = (bf16[2,1,128,2,128]{2,4,0,3,1:T(8,128)(2,1)}, bf16[2,1,128,2,128]{2,4,0,3,1:T(8,128)(2,1)S(1)}, u32[]{:S(2)}, u32[]{:S(2)}) collective-permute-start(bf16[2,1,128,2,128]{2,4,0,3,1:T(8,128)(2,1)} %pad_maximum_fusion.2), channel_id=1, source_target_pairs={{0,32},{16,48},{32,0},{48,16},{64,96},{80,112},{96,64},{112,80},{1... | collective-permute-start | bytes 393224 | tf_op jit(solution)/shard_map/ppermute | solution.py:22
  74.0 30.5 %collective-permute-start.8 = (bf16[2,1,128,2,128]{2,4,0,3,1:T(8,128)(2,1)}, bf16[2,1,128,2,128]{2,4,0,3,1:T(8,128)(2,1)}, u32[]{:S(2)}, u32[]{:S(2)}) collective-permute-start(bf16[2,1,128,2,128]{2,4,0,3,1:T(8,128)(2,1)} %pad_maximum_fusion.3), channel_id=1, source_target_pairs={{0,64},{16,80},{32,96},{48,112},{64,0},{80,16},{96,32},{112,48},{1... | collective-permute-start | bytes 393224 | tf_op jit(solution)/shard_map/ppermute | solution.py:22
  79.7 24.8 %collective-permute-start.9 = (bf16[2,1,128,2,128]{2,4,0,3,1:T(8,128)(2,1)}, bf16[2,1,128,2,128]{2,4,0,3,1:T(8,128)(2,1)}, u32[]{:S(2)}, u32[]{:S(2)}) collective-permute-start(bf16[2,1,128,2,128]{2,4,0,3,1:T(8,128)(2,1)} %pad_maximum_fusion.4), channel_id=1, source_target_pairs={{0,128},{16,144},{32,160},{48,176},{64,192},{80,208},{96,224},{112... | collective-permute-start | bytes 393224 | tf_op jit(solution)/shard_map/ppermute | solution.py:22
  83.6 21.0 %collective-permute-start.10 = (bf16[2,1,128,2,128]{2,4,0,3,1:T(8,128)(2,1)}, bf16[2,1,128,2,128]{2,4,0,3,1:T(8,128)(2,1)}, u32[]{:S(2)}, u32[]{:S(2)}) collective-permute-start(bf16[2,1,128,2,128]{2,4,0,3,1:T(8,128)(2,1)} %pad_maximum_fusion.5), channel_id=1, source_target_pairs={{0,256},{16,272},{32,288},{48,304},{64,320},{80,336},{96,352},{112... | collective-permute-start | bytes 393224 | tf_op jit(solution)/shard_map/ppermute | solution.py:22
  88.6 16.0 %collective-permute-start.11 = (bf16[2,1,128,2,128]{2,4,0,3,1:T(8,128)(2,1)}, bf16[2,1,128,2,128]{2,4,0,3,1:T(8,128)(2,1)}, u32[]{:S(2)}, u32[]{:S(2)}) collective-permute-start(bf16[2,1,128,2,128]{2,4,0,3,1:T(8,128)(2,1)} %pad_maximum_fusion.6), channel_id=1, source_target_pairs={{0,512},{16,528},{32,544},{48,560},{64,576},{80,592},{96,608},{112... | collective-permute-start | bytes 393224 | tf_op jit(solution)/shard_map/ppermute | solution.py:22
  97.8 14.8 %all-to-all-start.1 = ((bf16[8,64,128]{2,1,0:T(8,128)(2,1)}), bf16[8,64,128]{2,1,0:T(8,128)(2,1)S(1)}, u32[]{:S(2)}, u32[]{:S(2)}) async-start(bf16[8,64,128]{2,1,0:T(8,128)(2,1)} %reduce_sum.41), calls=%async_computation.1 | async-start | bytes 262144 | tf_op jit(solution)/shard_map/all_to_all | solution.py:83
  101.2 6.3 %collective-permute-start.6 = (bf16[2,1,128,2,128]{2,4,0,3,1:T(8,128)(2,1)}, bf16[2,1,128,2,128]{2,4,0,3,1:T(8,128)(2,1)S(1)}, u32[]{:S(2)}, u32[]{:S(2)}) collective-permute-start(bf16[2,1,128,2,128]{2,4,0,3,1:T(8,128)(2,1)} %pad_maximum_fusion.1), channel_id=1, source_target_pairs={{0,16},{16,0},{32,48},{48,32},{64,80},{80,64},{96,112},{112,96},{1... | collective-permute-start | bytes 393224 | tf_op jit(solution)/shard_map/ppermute | solution.py:22
Sparse Core Ops, SparseCore 0:
  40.6 24.9 all-gather.1

commit v4 on v3

--- a/solution.py
+++ b/solution.py
@@ -54,11 +54,19 @@
         "shtmu,msuhc->sthc", probs_low, value_near, preferred_element_type=jnp.float32
     ).astype(jnp.bfloat16)
     grad_rows = grad_out.reshape(local_seqs * block_len, D)
-    grad_rows_other = swapped(grad_rows, "fsdp", 0)
+    w_rows = w_out.shape[0]
+    inputs_out = jnp.concatenate([grad_rows.reshape(-1, w_out.shape[1]), w_out], axis=0)
+    inputs_in = swapped(inputs_out, "fsdp", 0)
+    grad_rows_other = inputs_in[:-w_rows].reshape(grad_rows.shape)
+    w_other = inputs_in[-w_rows:]
     columns = grad_rows
+    w_first = lax.axis_index("fsdp") == 0
+    w_full = jnp.where(
+        w_first, jnp.concatenate([w_out, w_other], axis=1), jnp.concatenate([w_other, w_out], axis=1)
+    )
     grad_att = lax.dot_general(
         columns,
-        lax.all_gather(w_out, "fsdp", axis=1, tiled=True),
+        w_full,
         (((1,), (1,)), ((), ())),
         preferred_element_type=jnp.float32,
     ).astype(jnp.bfloat16)

time: 121 us -> 132 us (1.091)
  the two profiles are of different devices: /device:TPU:1 before, /device:TPU:28 now
where the time goes in v4:
time: 132 us; the launch traced here: 131 us
  starting transfers between devices  84.4 us (64%)
  local copies, waits for them, and re-layouts  22.7 us (17%)
  other arithmetic  10.2 us (8%)
  matrix products  6.81 us (5%)
  waiting for transfers between devices  5.69 us (4%)
    ppermute x14, starting transfers between devices, swapped(): lax.ppermute(shard, axis, [(i, i ^ 1 << distance) for i in range(size_of(...  64.3 us
    all_to_all x1, starting transfers between devices, per_device_body(): lax.all_to_all(inner.astype(jnp.bfloat16), 'seq_hi', 0, 0, tiled=False)  14.9 us
    another operation x7, local copies, waits for them, and re-layouts, per_device_body(): jnp.stack(collected)  7.46 us
    unnamed x36, local copies, waits for them, and re-layouts  7.11 us
    all_to_all x1, starting transfers between devices, per_device_body(): lax.all_to_all(pieces.astype(jnp.bfloat16), 'seq_lo', 1, 1, tiled=False)  5.23 us
    ppermute x14, waiting for transfers between devices, swapped(): lax.ppermute(shard, axis, [(i, i ^ 1 << distance) for i in range(size_of(...  4.06 us
    another operation x6, other arithmetic, per_device_body(): jnp.stack([key_terms[level + 1], value_terms[level + 1]])  3.95 us
  transfers between devices with their start and end apart: 16, of which 2 were waited for; matrix products, arithmetic and copies ran while one was open for 24% of the time, Pallas kernels for 0%

profile of v4, /device:TPU:28, one launch (start us, length us, event | category | flops | bytes accessed | tf_op | source)
XLA Modules:
  0.0 131.0 jit_solution(6884643946441763120)
XLA Ops:
  3.2 2.3 %collective-permute-start = (bf16[2,1,128,256]{2,3,0,1:T(8,128)(2,1)}, bf16[2,1,128,256]{2,3,0,1:T(8,128)(2,1)S(1)}, u32[]{:S(2)}, u32[]{:S(2)}) collective-permute-start(bf16[2,1,128,256]{2,3,0,1:T(8,128)(2,1)} %pad_maximum_fusion.1), channel_id=1, source_target_pairs={{0,16},{16,0},{32,48},{48,32},{64,80},{80,64},{96,112},{112,96},{1... | collective-permute-start | bytes 393224 | tf_op jit(solution)/shard_map/ppermute | solution.py:22
  5.6 2.2 %collective-permute-start.1 = (bf16[2,1,128,256]{2,3,0,1:T(8,128)(2,1)}, bf16[2,1,128,256]{2,3,0,1:T(8,128)(2,1)}, u32[]{:S(2)}, u32[]{:S(2)}) collective-permute-start(bf16[2,1,128,256]{2,3,0,1:T(8,128)(2,1)} %pad_maximum_fusion.1), channel_id=1, source_target_pairs={{0,32},{16,48},{32,0},{48,16},{64,96},{80,112},{96,64},{112,80},{1... | collective-permute-start | bytes 393224 | tf_op jit(solution)/shard_map/ppermute | solution.py:22
  7.8 7.7 %collective-permute-start.2 = (bf16[2,1,128,256]{2,3,0,1:T(8,128)(2,1)}, bf16[2,1,128,256]{2,3,0,1:T(8,128)(2,1)}, u32[]{:S(2)}, u32[]{:S(2)}) collective-permute-start(bf16[2,1,128,256]{2,3,0,1:T(8,128)(2,1)} %pad_maximum_fusion.1), channel_id=1, source_target_pairs={{0,64},{16,80},{32,96},{48,112},{64,0},{80,16},{96,32},{112,48},{1... | collective-permute-start | bytes 393224 | tf_op jit(solution)/shard_map/ppermute | solution.py:22
  15.6 4.3 %collective-permute-start.3 = (bf16[2,1,128,256]{2,3,0,1:T(8,128)(2,1)}, bf16[2,1,128,256]{2,3,0,1:T(8,128)(2,1)S(1)}, u32[]{:S(2)}, u32[]{:S(2)}) collective-permute-start(bf16[2,1,128,256]{2,3,0,1:T(8,128)(2,1)} %pad_maximum_fusion.1), channel_id=1, source_target_pairs={{0,128},{16,144},{32,160},{48,176},{64,192},{80,208},{96,224},{112... | collective-permute-start | bytes 393224 | tf_op jit(solution)/shard_map/ppermute | solution.py:22
  19.9 1.4 %reshape_reshape.3 = bf16[256,2048]{1,0:T(8,128)(2,1)S(1)} reshape(bf16[1,128,4096]{2,1,0:T(8,128)(2,1)} %param.9) | data formatting | bytes 2097152 | tf_op jit(solution)/shard_map/reshape;reshape | solution.py:58
  22.7 1.9 %collective-permute-start.6 = (bf16[512,2048]{1,0:T(8,128)(2,1)S(1)}, bf16[512,2048]{1,0:T(8,128)(2,1)}, u32[]{:S(2)}, u32[]{:S(2)}) collective-permute-start(bf16[512,2048]{1,0:T(8,128)(2,1)S(1)} %pad_maximum_fusion), channel_id=1, source_target_pairs={{0,1},{1,0},{2,3},{3,2},{4,5},{5,4},{6,7},{7,6},{8,9},{9,8},{10,11... | collective-permute-start | bytes 6291464 | tf_op jit(solution)/shard_map/ppermute | solution.py:22
  24.8 6.1 %collective-permute-start.4 = (bf16[2,1,128,256]{2,3,0,1:T(8,128)(2,1)}, bf16[2,1,128,256]{2,3,0,1:T(8,128)(2,1)}, u32[]{:S(2)}, u32[]{:S(2)}) collective-permute-start(bf16[2,1,128,256]{2,3,0,1:T(8,128)(2,1)} %pad_maximum_fusion.1), channel_id=1, source_target_pairs={{0,256},{16,272},{32,288},{48,304},{64,320},{80,336},{96,352},{112... | collective-permute-start | bytes 393224 | tf_op jit(solution)/shard_map/ppermute | solution.py:22
  30.9 10.9 %collective-permute-start.5 = (bf16[2,1,128,256]{2,3,0,1:T(8,128)(2,1)}, bf16[2,1,128,256]{2,3,0,1:T(8,128)(2,1)}, u32[]{:S(2)}, u32[]{:S(2)}) collective-permute-start(bf16[2,1,128,256]{2,3,0,1:T(8,128)(2,1)} %pad_maximum_fusion.1), channel_id=1, source_target_pairs={{0,512},{16,528},{32,544},{48,560},{64,576},{80,592},{96,608},{112... | collective-permute-start | bytes 393224 | tf_op jit(solution)/shard_map/ppermute | solution.py:22
  48.4 1.7 %copy.81 = bf16[1,2,1,128,2,128]{5,3,0,4,2,1:T(8,128)(2,1)} copy(bf16[1,2,1,128,2,128]{3,5,4,1,2,0:T(8,128)(2,1)} %bitcast.8) | data formatting | bytes 262144 | tf_op jit(solution)/shard_map/stack | solution.py:35
  50.1 1.7 %copy.82 = bf16[1,2,1,128,2,128]{5,3,0,4,2,1:T(8,128)(2,1)} copy(bf16[1,2,1,128,2,128]{3,5,4,1,2,0:T(8,128)(2,1)} %bitcast.9) | data formatting | bytes 262144 | tf_op jit(solution)/shard_map/stack | solution.py:35
  57.4 2.1 %collective-permute-start.13 = (bf16[128,128]{0,1:T(8,128)(2,1)S(1)}, bf16[128,128]{0,1:T(8,128)(2,1)S(1)}, u32[]{:S(2)}, u32[]{:S(2)}) collective-permute-start(bf16[128,128]{0,1:T(8,128)(2,1)S(1)} %get-tuple-element.37), channel_id=1, source_target_pairs={{0,1},{1,0},{2,3},{3,2},{4,5},{5,4},{6,7},{7,6},{8,9},{9,8},{10,11... | collective-permute-start | bytes 98312 | tf_op jit(solution)/shard_map/ppermute | solution.py:22
  59.5 1.7 %fusion.41 = (bf16[256,2048]{1,0:T(8,128)(2,1)S(1)}, bf16[256,2048]{1,0:T(8,128)(2,1)S(1)}) fusion(bf16[512,2048]{1,0:T(8,128)(2,1)} %collective-permute-done.6), kind=kLoop, calls=%fused_computation.75 | loop fusion | bytes 4194304 | tf_op jit(solution)/shard_map/slice | solution.py:60
  62.0 1.4 %fusion.45 = (bf16[7,1,128,2,128]{2,4,0,3,1:T(8,128)(2,1)}, f32[7,1,128,2,128]{2,4,0,3,1:T(8,128)}) fusion(bf16[128,2,128,1]{0,2,3,1:T(8,128)(2,1)S(1)} %bitcast.97, f32[2,128]{1,0:T(2,128)S(1)} %fusion.16, f32[2,128,7,128]{1,3,2,0:T(8,128)S(1)} %get-tuple-element.39, f32[2,128]{1,0:T(2,128)S(1)} %get-tuple-element.38), kind=kOutput, calls=%fused_computation.79 | convolution fusion | flops 59637760 | bytes 2361344 | tf_op jit(solution)/shard_map/shtmu,sthc->msuhc/dot_general | solution.py:104
  64.6 2.0 %convolution_convert_fusion = bf16[4096,128]{1,0:T(8,128)(2,1)S(1)} fusion(bf16[128,4096]{1,0:T(8,128)(2,1)} %reshape.560, bf16[128,4096]{1,0:T(8,128)(2,1)S(1)} %bitcast.85, bf16[128,128]{0,1:T(8,128)(2,1)S(1)} %collective-permute-done.13, bf16[128,128]{0,1:T(8,128)(2,1)S(1)} %get-tuple-element.36), kind=kOutput, calls=%fused_computation | convolution fusion | flops 273285120 | bytes 3211264 | tf_op jit(solution)/shard_map/dot_general | solution.py:83
  67.7 5.2 %all-to-all-start = ((bf16[8,8,64,128]{3,2,0,1:T(8,128)(2,1)}), bf16[8,8,64,128]{3,2,0,1:T(8,128)(2,1)S(1)}, u32[]{:S(2)}, u32[]{:S(2)}) async-start(bf16[8,8,64,128]{3,2,0,1:T(8,128)(2,1)} %copy.92), calls=%async_computation | async-start | bytes 2097152 | tf_op jit(solution)/shard_map/all_to_all | solution.py:89
  75.1 3.7 %collective-permute-start.12 = (bf16[2,1,128,2,128]{2,4,0,3,1:T(8,128)(2,1)}, bf16[2,1,128,2,128]{2,4,0,3,1:T(8,128)(2,1)S(1)}, u32[]{:S(2)}, u32[]{:S(2)}) collective-permute-start(bf16[2,1,128,2,128]{2,4,0,3,1:T(8,128)(2,1)} %pad_maximum_fusion.7), channel_id=1, source_target_pairs={{0,512},{16,528},{32,544},{48,560},{64,576},{80,592},{96,608},{112... | collective-permute-start | bytes 393224 | tf_op jit(solution)/shard_map/ppermute | solution.py:22
  79.4 7.7 %collective-permute-start.11 = (bf16[2,1,128,2,128]{2,4,0,3,1:T(8,128)(2,1)}, bf16[2,1,128,2,128]{2,4,0,3,1:T(8,128)(2,1)}, u32[]{:S(2)}, u32[]{:S(2)}) collective-permute-start(bf16[2,1,128,2,128]{2,4,0,3,1:T(8,128)(2,1)} %pad_maximum_fusion.6), channel_id=1, source_target_pairs={{0,256},{16,272},{32,288},{48,304},{64,320},{80,336},{96,352},{112... | collective-permute-start | bytes 393224 | tf_op jit(solution)/shard_map/ppermute | solution.py:22
  87.8 4.6 %collective-permute-start.10 = (bf16[2,1,128,2,128]{2,4,0,3,1:T(8,128)(2,1)}, bf16[2,1,128,2,128]{2,4,0,3,1:T(8,128)(2,1)}, u32[]{:S(2)}, u32[]{:S(2)}) collective-permute-start(bf16[2,1,128,2,128]{2,4,0,3,1:T(8,128)(2,1)} %pad_maximum_fusion.5), channel_id=1, source_target_pairs={{0,128},{16,144},{32,160},{48,176},{64,192},{80,208},{96,224},{112... | collective-permute-start | bytes 393224 | tf_op jit(solution)/shard_map/ppermute | solution.py:22
  93.1 4.6 %collective-permute-start.9 = (bf16[2,1,128,2,128]{2,4,0,3,1:T(8,128)(2,1)}, bf16[2,1,128,2,128]{2,4,0,3,1:T(8,128)(2,1)}, u32[]{:S(2)}, u32[]{:S(2)}) collective-permute-start(bf16[2,1,128,2,128]{2,4,0,3,1:T(8,128)(2,1)} %pad_maximum_fusion.4), channel_id=1, source_target_pairs={{0,64},{16,80},{32,96},{48,112},{64,0},{80,16},{96,32},{112,48},{1... | collective-permute-start | bytes 393224 | tf_op jit(solution)/shard_map/ppermute | solution.py:22
  98.3 4.3 %collective-permute-start.8 = (bf16[2,1,128,2,128]{2,4,0,3,1:T(8,128)(2,1)}, bf16[2,1,128,2,128]{2,4,0,3,1:T(8,128)(2,1)}, u32[]{:S(2)}, u32[]{:S(2)}) collective-permute-start(bf16[2,1,128,2,128]{2,4,0,3,1:T(8,128)(2,1)} %pad_maximum_fusion.3), channel_id=1, source_target_pairs={{0,32},{16,48},{32,0},{48,16},{64,96},{80,112},{96,64},{112,80},{1... | collective-permute-start | bytes 393224 | tf_op jit(solution)/shard_map/ppermute | solution.py:22
  104.0 14.9 %all-to-all-start.1 = ((bf16[8,64,128]{2,1,0:T(8,128)(2,1)}), bf16[8,64,128]{2,1,0:T(8,128)(2,1)S(1)}, u32[]{:S(2)}, u32[]{:S(2)}) async-start(bf16[8,64,128]{2,1,0:T(8,128)(2,1)} %reduce_sum.41), calls=%async_computation.1 | async-start | bytes 262144 | tf_op jit(solution)/shard_map/all_to_all | solution.py:91
  118.9 1.9 %collective-permute-start.7 = (bf16[2,1,128,2,128]{2,4,0,3,1:T(8,128)(2,1)}, bf16[2,1,128,2,128]{2,4,0,3,1:T(8,128)(2,1)S(1)}, u32[]{:S(2)}, u32[]{:S(2)}) collective-permute-start(bf16[2,1,128,2,128]{2,4,0,3,1:T(8,128)(2,1)} %pad_maximum_fusion.2), channel_id=1, source_target_pairs={{0,16},{16,0},{32,48},{48,32},{64,80},{80,64},{96,112},{112,96},{1... | collective-permute-start | bytes 393224 | tf_op jit(solution)/shard_map/ppermute | solution.py:22
  122.0 4.0 %collective-permute-done.7 = bf16[2,1,128,2,128]{2,4,0,3,1:T(8,128)(2,1)S(1)} collective-permute-done((bf16[2,1,128,2,128]{2,4,0,3,1:T(8,128)(2,1)}, bf16[2,1,128,2,128]{2,4,0,3,1:T(8,128)(2,1)S(1)}, u32[]{:S(2)}, u32[]{:S(2)}) %collective-permute-start.7) | collective-permute-done | bytes 131104 | tf_op jit(solution)/shard_map/ppermute | solution.py:22
  128.7 1.6 %all-to-all-done.1 = bf16[8,64,128]{2,1,0:T(8,128)(2,1)S(1)} async-done(((bf16[8,64,128]{2,1,0:T(8,128)(2,1)}), bf16[8,64,128]{2,1,0:T(8,128)(2,1)S(1)}, u32[]{:S(2)}, u32[]{:S(2)}) %all-to-all-start.1) | async-done | bytes 131104 | tf_op jit(solution)/shard_map/all_to_all | solution.py:91
  (90 shorter events, 29.9 us)
Async XLA Ops:
  3.2 21.5 %collective-permute-start = (bf16[2,1,128,256]{2,3,0,1:T(8,128)(2,1)}, bf16[2,1,128,256]{2,3,0,1:T(8,128)(2,1)S(1)}, u32[]{:S(2)}, u32[]{:S(2)}) collective-permute-start(bf16[2,1,128,256]{2,3,0,1:T(8,128)(2,1)} %pad_maximum_fusion.1), channel_id=1, source_target_pairs={{0,16},{16,0},{32,48},{48,32},{64,80},{80,64},{96,112},{112,96},{1... | collective-permute-start | bytes 393224 | tf_op jit(solution)/shard_map/ppermute | solution.py:22
  5.6 25.3 %collective-permute-start.1 = (bf16[2,1,128,256]{2,3,0,1:T(8,128)(2,1)}, bf16[2,1,128,256]{2,3,0,1:T(8,128)(2,1)}, u32[]{:S(2)}, u32[]{:S(2)}) collective-permute-start(bf16[2,1,128,256]{2,3,0,1:T(8,128)(2,1)} %pad_maximum_fusion.1), channel_id=1, source_target_pairs={{0,32},{16,48},{32,0},{48,16},{64,96},{80,112},{96,64},{112,80},{1... | collective-permute-start | bytes 393224 | tf_op jit(solution)/shard_map/ppermute | solution.py:22
  7.8 37.8 %collective-permute-start.2 = (bf16[2,1,128,256]{2,3,0,1:T(8,128)(2,1)}, bf16[2,1,128,256]{2,3,0,1:T(8,128)(2,1)}, u32[]{:S(2)}, u32[]{:S(2)}) collective-permute-start(bf16[2,1,128,256]{2,3,0,1:T(8,128)(2,1)} %pad_maximum_fusion.1), channel_id=1, source_target_pairs={{0,64},{16,80},{32,96},{48,112},{64,0},{80,16},{96,32},{112,48},{1... | collective-permute-start | bytes 393224 | tf_op jit(solution)/shard_map/ppermute | solution.py:22
  15.6 31.1 %collective-permute-start.3 = (bf16[2,1,128,256]{2,3,0,1:T(8,128)(2,1)}, bf16[2,1,128,256]{2,3,0,1:T(8,128)(2,1)S(1)}, u32[]{:S(2)}, u32[]{:S(2)}) collective-permute-start(bf16[2,1,128,256]{2,3,0,1:T(8,128)(2,1)} %pad_maximum_fusion.1), channel_id=1, source_target_pairs={{0,128},{16,144},{32,160},{48,176},{64,192},{80,208},{96,224},{112... | collective-permute-start | bytes 393224 | tf_op jit(solution)/shard_map/ppermute | solution.py:22
  21.3 3.4 %copy-start.12 = (s32[1,6]{1,0:T(1,128)S(1)}, s32[1,6]{1,0:T(1,128)}, u32[]{:S(2)}) copy-start(s32[1,6]{1,0:T(1,128)} %param.11) | copy-start | bytes 76
  22.7 36.8 %collective-permute-start.6 = (bf16[512,2048]{1,0:T(8,128)(2,1)S(1)}, bf16[512,2048]{1,0:T(8,128)(2,1)}, u32[]{:S(2)}, u32[]{:S(2)}) collective-permute-start(bf16[512,2048]{1,0:T(8,128)(2,1)S(1)} %pad_maximum_fusion), channel_id=1, source_target_pairs={{0,1},{1,0},{2,3},{3,2},{4,5},{5,4},{6,7},{7,6},{8,9},{9,8},{10,11... | collective-permute-start | bytes 6291464 | tf_op jit(solution)/shard_map/ppermute | solution.py:22
  24.8 23.6 %collective-permute-start.4 = (bf16[2,1,128,256]{2,3,0,1:T(8,128)(2,1)}, bf16[2,1,128,256]{2,3,0,1:T(8,128)(2,1)}, u32[]{:S(2)}, u32[]{:S(2)}) collective-permute-start(bf16[2,1,128,256]{2,3,0,1:T(8,128)(2,1)} %pad_maximum_fusion.1), channel_id=1, source_target_pairs={{0,256},{16,272},{32,288},{48,304},{64,320},{80,336},{96,352},{112... | collective-permute-start | bytes 393224 | tf_op jit(solution)/shard_map/ppermute | solution.py:22
  30.9 19.2 %collective-permute-start.5 = (bf16[2,1,128,256]{2,3,0,1:T(8,128)(2,1)}, bf16[2,1,128,256]{2,3,0,1:T(8,128)(2,1)}, u32[]{:S(2)}, u32[]{:S(2)}) collective-permute-start(bf16[2,1,128,256]{2,3,0,1:T(8,128)(2,1)} %pad_maximum_fusion.1), channel_id=1, source_target_pairs={{0,512},{16,528},{32,544},{48,560},{64,576},{80,592},{96,608},{112... | collective-permute-start | bytes 393224 | tf_op jit(solution)/shard_map/ppermute | solution.py:22
  51.7 3.7 %copy-start.8 = (bf16[128,2,128,1]{0,2,3,1:T(8,128)(2,1)S(1)}, bf16[128,2,128,1]{0,2,3,1:T(8,128)(2,1)}, u32[]{:S(2)}) copy-start(bf16[128,2,128,1]{0,2,3,1:T(8,128)(2,1)} %copy.102) | copy-start | bytes 196612
  51.7 3.7 %copy-start.11 = (pred[128,7,128]{0,2,1:T(8,128)(4,1)S(1)}, pred[128,7,128]{0,2,1:T(8,128)(4,1)}, u32[]{:S(2)}) copy-start(pred[128,7,128]{0,2,1:T(8,128)(4,1)} %broadcast_select_fusion) | copy-start | bytes 344068
  57.4 3.8 %copy-start.4 = (bf16[1,128,4096]{2,1,0:T(8,128)(2,1)S(1)}, bf16[1,128,4096]{2,1,0:T(8,128)(2,1)}, u32[]{:S(2)}) copy-start(bf16[1,128,4096]{2,1,0:T(8,128)(2,1)} %param.9) | copy-start | bytes 3145732
  57.4 3.8 %copy-start.6 = (bf16[256,2048]{1,0:T(8,128)(2,1)S(1)}, bf16[256,2048]{1,0:T(8,128)(2,1)}, u32[]{:S(2)}) copy-start(bf16[256,2048]{1,0:T(8,128)(2,1)} %param.10) | copy-start | bytes 3145732
  57.4 7.1 %collective-permute-start.13 = (bf16[128,128]{0,1:T(8,128)(2,1)S(1)}, bf16[128,128]{0,1:T(8,128)(2,1)S(1)}, u32[]{:S(2)}, u32[]{:S(2)}) collective-permute-start(bf16[128,128]{0,1:T(8,128)(2,1)S(1)} %get-tuple-element.37), channel_id=1, source_target_pairs={{0,1},{1,0},{2,3},{3,2},{4,5},{5,4},{6,7},{7,6},{8,9},{9,8},{10,11... | collective-permute-start | bytes 98312 | tf_op jit(solution)/shard_map/ppermute | solution.py:22
  66.6 6.3 %copy-start = (bf16[7,1,1,128,2,128]{5,3,0,4,2,1:T(8,128)(2,1)S(1)}, bf16[7,1,1,128,2,128]{5,3,0,4,2,1:T(8,128)(2,1)}, u32[]{:S(2)}) copy-start(bf16[7,1,1,128,2,128]{5,3,0,4,2,1:T(8,128)(2,1)} %slice.133) | copy-start | bytes 1376260
  67.7 5.5 %copy-start.7 = (bf16[7,1,128,2,128]{2,4,0,3,1:T(8,128)(2,1)S(1)}, bf16[7,1,128,2,128]{2,4,0,3,1:T(8,128)(2,1)}, u32[]{:S(2)}) copy-start(bf16[7,1,128,2,128]{2,4,0,3,1:T(8,128)(2,1)} %get-tuple-element.40) | copy-start | bytes 1376260
  67.7 35.5 %all-to-all-start = ((bf16[8,8,64,128]{3,2,0,1:T(8,128)(2,1)}), bf16[8,8,64,128]{3,2,0,1:T(8,128)(2,1)S(1)}, u32[]{:S(2)}, u32[]{:S(2)}) async-start(bf16[8,8,64,128]{3,2,0,1:T(8,128)(2,1)} %copy.92), calls=%async_computation | async-start | bytes 2097152 | tf_op jit(solution)/shard_map/all_to_all | solution.py:89
  74.4 46.5 %copy-start.3 = (bf16[7,2,1,128,2,128]{5,3,0,4,2,1:T(8,128)(2,1)S(1)}, bf16[7,2,1,128,2,128]{5,3,0,4,2,1:T(8,128)(2,1)}, u32[]{:S(2)}) copy-start(bf16[7,2,1,128,2,128]{5,3,0,4,2,1:T(8,128)(2,1)} %copy-done.1) | copy-start | bytes 2752516
  75.1 43.9 %collective-permute-start.12 = (bf16[2,1,128,2,128]{2,4,0,3,1:T(8,128)(2,1)}, bf16[2,1,128,2,128]{2,4,0,3,1:T(8,128)(2,1)S(1)}, u32[]{:S(2)}, u32[]{:S(2)}) collective-permute-start(bf16[2,1,128,2,128]{2,4,0,3,1:T(8,128)(2,1)} %pad_maximum_fusion.7), channel_id=1, source_target_pairs={{0,512},{16,528},{32,544},{48,560},{64,576},{80,592},{96,608},{112... | collective-permute-start | bytes 393224 | tf_op jit(solution)/shard_map/ppermute | solution.py:22
  79.4 42.6 %collective-permute-start.11 = (bf16[2,1,128,2,128]{2,4,0,3,1:T(8,128)(2,1)}, bf16[2,1,128,2,128]{2,4,0,3,1:T(8,128)(2,1)}, u32[]{:S(2)}, u32[]{:S(2)}) collective-permute-start(bf16[2,1,128,2,128]{2,4,0,3,1:T(8,128)(2,1)} %pad_maximum_fusion.6), channel_id=1, source_target_pairs={{0,256},{16,272},{32,288},{48,304},{64,320},{80,336},{96,352},{112... | collective-permute-start | bytes 393224 | tf_op jit(solution)/shard_map/ppermute | solution.py:22
  87.8 34.2 %collective-permute-start.10 = (bf16[2,1,128,2,128]{2,4,0,3,1:T(8,128)(2,1)}, bf16[2,1,128,2,128]{2,4,0,3,1:T(8,128)(2,1)}, u32[]{:S(2)}, u32[]{:S(2)}) collective-permute-start(bf16[2,1,128,2,128]{2,4,0,3,1:T(8,128)(2,1)} %pad_maximum_fusion.5), channel_id=1, source_target_pairs={{0,128},{16,144},{32,160},{48,176},{64,192},{80,208},{96,224},{112... | collective-permute-start | bytes 393224 | tf_op jit(solution)/shard_map/ppermute | solution.py:22
  93.1 28.9 %collective-permute-start.9 = (bf16[2,1,128,2,128]{2,4,0,3,1:T(8,128)(2,1)}, bf16[2,1,128,2,128]{2,4,0,3,1:T(8,128)(2,1)}, u32[]{:S(2)}, u32[]{:S(2)}) collective-permute-start(bf16[2,1,128,2,128]{2,4,0,3,1:T(8,128)(2,1)} %pad_maximum_fusion.4), channel_id=1, source_target_pairs={{0,64},{16,80},{32,96},{48,112},{64,0},{80,16},{96,32},{112,48},{1... | collective-permute-start | bytes 393224 | tf_op jit(solution)/shard_map/ppermute | solution.py:22
  98.3 23.7 %collective-permute-start.8 = (bf16[2,1,128,2,128]{2,4,0,3,1:T(8,128)(2,1)}, bf16[2,1,128,2,128]{2,4,0,3,1:T(8,128)(2,1)}, u32[]{:S(2)}, u32[]{:S(2)}) collective-permute-start(bf16[2,1,128,2,128]{2,4,0,3,1:T(8,128)(2,1)} %pad_maximum_fusion.3), channel_id=1, source_target_pairs={{0,32},{16,48},{32,0},{48,16},{64,96},{80,112},{96,64},{112,80},{1... | collective-permute-start | bytes 393224 | tf_op jit(solution)/shard_map/ppermute | solution.py:22
  104.0 26.3 %all-to-all-start.1 = ((bf16[8,64,128]{2,1,0:T(8,128)(2,1)}), bf16[8,64,128]{2,1,0:T(8,128)(2,1)S(1)}, u32[]{:S(2)}, u32[]{:S(2)}) async-start(bf16[8,64,128]{2,1,0:T(8,128)(2,1)} %reduce_sum.41), calls=%async_computation.1 | async-start | bytes 262144 | tf_op jit(solution)/shard_map/all_to_all | solution.py:91
  118.9 7.1 %collective-permute-start.7 = (bf16[2,1,128,2,128]{2,4,0,3,1:T(8,128)(2,1)}, bf16[2,1,128,2,128]{2,4,0,3,1:T(8,128)(2,1)S(1)}, u32[]{:S(2)}, u32[]{:S(2)}) collective-permute-start(bf16[2,1,128,2,128]{2,4,0,3,1:T(8,128)(2,1)} %pad_maximum_fusion.2), channel_id=1, source_target_pairs={{0,16},{16,0},{32,48},{48,32},{64,80},{80,64},{96,112},{112,96},{1... | collective-permute-start | bytes 393224 | tf_op jit(solution)/shard_map/ppermute | solution.py:22
  (5 other events, 6.6 us)

commit v5 on v4

--- a/solution.py
+++ b/solution.py
@@ -54,12 +54,9 @@
         "shtmu,msuhc->sthc", probs_low, value_near, preferred_element_type=jnp.float32
     ).astype(jnp.bfloat16)
     grad_rows = grad_out.reshape(local_seqs * block_len, D)
-    w_rows = w_out.shape[0]
-    inputs_out = jnp.concatenate([grad_rows.reshape(-1, w_out.shape[1]), w_out], axis=0)
-    inputs_in = swapped(inputs_out, "fsdp", 0)
-    grad_rows_other = inputs_in[:-w_rows].reshape(grad_rows.shape)
-    w_other = inputs_in[-w_rows:]
+    grad_rows_other = swapped(grad_rows, "fsdp", 0)
     columns = grad_rows
+    w_other = swapped(w_out, "fsdp", 0)
     w_first = lax.axis_index("fsdp") == 0
     w_full = jnp.where(
         w_first, jnp.concatenate([w_out, w_other], axis=1), jnp.concatenate([w_other, w_out], axis=1)

time: 132 us -> 110 us (0.83)
  the two profiles are of different devices: /device:TPU:28 before, /device:TPU:24 now
where the time goes in v5:
time: 110 us; the launch traced here: 109 us
  starting transfers between devices  71.1 us (65%)
  waiting for transfers between devices  13 us (12%)
  matrix products  8.54 us (8%)
  other arithmetic  8.23 us (7%)
  local copies, waits for them, and re-layouts  7.44 us (7%)
    ppermute x15, starting transfers between devices, swapped(): lax.ppermute(shard, axis, [(i, i ^ 1 << distance) for i in range(size_of(...  61.1 us
    all_to_all x1, waiting for transfers between devices, per_device_body(): lax.all_to_all(pieces.astype(jnp.bfloat16), 'seq_lo', 1, 1, tiled=False)  6.18 us
    ppermute x15, waiting for transfers between devices, swapped(): lax.ppermute(shard, axis, [(i, i ^ 1 << distance) for i in range(size_of(...  5.19 us
    all_to_all x1, starting transfers between devices, per_device_body(): lax.all_to_all(pieces.astype(jnp.bfloat16), 'seq_lo', 1, 1, tiled=False)  5.1 us
    all_to_all x1, starting transfers between devices, per_device_body(): lax.all_to_all(inner.astype(jnp.bfloat16), 'seq_hi', 0, 0, tiled=False)  4.94 us
    unnamed x10, local copies, waits for them, and re-layouts  4.23 us
    another operation x6, other arithmetic, per_device_body(): jnp.stack([key_terms[level + 1], value_terms[level + 1]])  4.01 us
    dot_general x1, matrix products, per_device_body(): lax.dot_general(columns, w_full, (((1,), (1,)), ((), ())), preferred_elem...  3.37 us
  transfers between devices with their start and end apart: 17, of which 4 were waited for; matrix products, arithmetic and copies ran while one was open for 20% of the time, Pallas kernels for 0%

profile of v5, /device:TPU:24, one launch (start us, length us, event | category | flops | bytes accessed | tf_op | source)
XLA Modules:
  0.0 109.4 jit_solution(3206940276494736866)
XLA Ops:
  2.6 10.9 %collective-permute-start.5 = (bf16[2,1,128,256]{2,3,0,1:T(8,128)(2,1)S(1)}, bf16[2,1,128,256]{2,3,0,1:T(8,128)(2,1)S(1)}, u32[]{:S(2)}, u32[]{:S(2)}) collective-permute-start(bf16[2,1,128,256]{2,3,0,1:T(8,128)(2,1)S(1)} %pad_maximum_fusion), channel_id=1, source_target_pairs={{0,512},{16,528},{32,544},{48,560},{64,576},{80,592},{96,608},{112... | collective-permute-start | bytes 393224 | tf_op jit(solution)/shard_map/ppermute | solution.py:22
  13.5 6.1 %collective-permute-start.4 = (bf16[2,1,128,256]{2,3,0,1:T(8,128)(2,1)S(1)}, bf16[2,1,128,256]{2,3,0,1:T(8,128)(2,1)S(1)}, u32[]{:S(2)}, u32[]{:S(2)}) collective-permute-start(bf16[2,1,128,256]{2,3,0,1:T(8,128)(2,1)S(1)} %pad_maximum_fusion), channel_id=1, source_target_pairs={{0,256},{16,272},{32,288},{48,304},{64,320},{80,336},{96,352},{112... | collective-permute-start | bytes 393224 | tf_op jit(solution)/shard_map/ppermute | solution.py:22
  19.6 4.3 %collective-permute-start.3 = (bf16[2,1,128,256]{2,3,0,1:T(8,128)(2,1)S(1)}, bf16[2,1,128,256]{2,3,0,1:T(8,128)(2,1)S(1)}, u32[]{:S(2)}, u32[]{:S(2)}) collective-permute-start(bf16[2,1,128,256]{2,3,0,1:T(8,128)(2,1)S(1)} %pad_maximum_fusion), channel_id=1, source_target_pairs={{0,128},{16,144},{32,160},{48,176},{64,192},{80,208},{96,224},{112... | collective-permute-start | bytes 393224 | tf_op jit(solution)/shard_map/ppermute | solution.py:22
  23.9 5.0 %collective-permute-start.2 = (bf16[2,1,128,256]{2,3,0,1:T(8,128)(2,1)S(1)}, bf16[2,1,128,256]{2,3,0,1:T(8,128)(2,1)S(1)}, u32[]{:S(2)}, u32[]{:S(2)}) collective-permute-start(bf16[2,1,128,256]{2,3,0,1:T(8,128)(2,1)S(1)} %pad_maximum_fusion), channel_id=1, source_target_pairs={{0,64},{16,80},{32,96},{48,112},{64,0},{80,16},{96,32},{112,48},{1... | collective-permute-start | bytes 393224 | tf_op jit(solution)/shard_map/ppermute | solution.py:22
  28.9 4.0 %collective-permute-start.1 = (bf16[2,1,128,256]{2,3,0,1:T(8,128)(2,1)S(1)}, bf16[2,1,128,256]{2,3,0,1:T(8,128)(2,1)S(1)}, u32[]{:S(2)}, u32[]{:S(2)}) collective-permute-start(bf16[2,1,128,256]{2,3,0,1:T(8,128)(2,1)S(1)} %pad_maximum_fusion), channel_id=1, source_target_pairs={{0,32},{16,48},{32,0},{48,16},{64,96},{80,112},{96,64},{112,80},{1... | collective-permute-start | bytes 393224 | tf_op jit(solution)/shard_map/ppermute | solution.py:22
  33.7 3.3 %collective-permute-start = (bf16[2,1,128,256]{2,3,0,1:T(8,128)(2,1)S(1)}, bf16[2,1,128,256]{2,3,0,1:T(8,128)(2,1)S(1)}, u32[]{:S(2)}, u32[]{:S(2)}) collective-permute-start(bf16[2,1,128,256]{2,3,0,1:T(8,128)(2,1)S(1)} %pad_maximum_fusion), channel_id=1, source_target_pairs={{0,16},{16,0},{32,48},{48,32},{64,80},{80,64},{96,112},{112,96},{1... | collective-permute-start | bytes 393224 | tf_op jit(solution)/shard_map/ppermute | solution.py:22
  38.6 1.9 %collective-permute-start.13 = (bf16[128,4096]{1,0:T(8,128)(2,1)}, bf16[128,4096]{1,0:T(8,128)(2,1)}, u32[]{:S(2)}, u32[]{:S(2)}) collective-permute-start(bf16[128,4096]{1,0:T(8,128)(2,1)} %bitcast.14), channel_id=1, source_target_pairs={{0,1},{1,0},{2,3},{3,2},{4,5},{5,4},{6,7},{7,6},{8,9},{9,8},{10,11... | collective-permute-start | bytes 3145736 | tf_op jit(solution)/shard_map/ppermute | solution.py:22
  40.6 2.4 %collective-permute-start.6 = (bf16[256,2048]{1,0:T(8,128)(2,1)}, bf16[256,2048]{1,0:T(8,128)(2,1)}, u32[]{:S(2)}, u32[]{:S(2)}) collective-permute-start(bf16[256,2048]{1,0:T(8,128)(2,1)} %param.10), channel_id=1, source_target_pairs={{0,1},{1,0},{2,3},{3,2},{4,5},{5,4},{6,7},{7,6},{8,9},{9,8},{10,11... | collective-permute-start | bytes 3145736 | tf_op jit(solution)/shard_map/ppermute | solution.py:22
  44.7 1.9 %collective-permute-start.14 = (bf16[128,128]{0,1:T(8,128)(2,1)S(1)}, bf16[128,128]{0,1:T(8,128)(2,1)S(1)}, u32[]{:S(2)}, u32[]{:S(2)}) collective-permute-start(bf16[128,128]{0,1:T(8,128)(2,1)S(1)} %get-tuple-element.35), channel_id=1, source_target_pairs={{0,1},{1,0},{2,3},{3,2},{4,5},{5,4},{6,7},{7,6},{8,9},{9,8},{10,11... | collective-permute-start | bytes 98312 | tf_op jit(solution)/shard_map/ppermute | solution.py:22
  47.8 2.3 %convolution_convert_fusion = bf16[4096,128]{1,0:T(8,128)(2,1)S(1)} fusion(bf16[128,4096]{1,0:T(8,128)(2,1)} %collective-permute-done.13, bf16[128,4096]{1,0:T(8,128)(2,1)} %bitcast.14, bf16[128,128]{0,1:T(8,128)(2,1)S(1)} %collective-permute-done.14, bf16[128,128]{0,1:T(8,128)(2,1)S(1)} %get-tuple-element.34), kind=kOutput, calls=%fused_computation | convolution fusion | flops 273285120 | bytes 3211264 | tf_op jit(solution)/shard_map/dot_general | solution.py:80
  51.1 5.1 %all-to-all-start = ((bf16[8,8,64,128]{3,2,0,1:T(8,128)(2,1)}), bf16[8,8,64,128]{3,2,0,1:T(8,128)(2,1)S(1)}, u32[]{:S(2)}, u32[]{:S(2)}) async-start(bf16[8,8,64,128]{3,2,0,1:T(8,128)(2,1)} %copy.92), calls=%async_computation | async-start | bytes 2097152 | tf_op jit(solution)/shard_map/all_to_all | solution.py:86
  56.2 3.4 %fusion.14 = bf16[256,128]{1,0:T(8,128)(2,1)S(1)} fusion(bf16[256,2048]{1,0:T(8,128)(2,1)} %collective-permute-done.6, bf16[256,2048]{1,0:T(8,128)(2,1)} %param.10, pred[]{:T(512)S(6)} %eq.11, bf16[1,128,4096]{2,1,0:T(8,128)(2,1)} %param.9), kind=kOutput, calls=%fused_computation.21 | convolution fusion | flops 277905408 | bytes 3211265 | tf_op jit(solution)/shard_map/dot_general | solution.py:64
  59.6 1.3 %fusion.44 = (bf16[7,1,128,2,128]{2,4,0,3,1:T(8,128)(2,1)S(1)}, f32[7,1,128,2,128]{2,4,0,3,1:T(8,128)}) fusion(bf16[128,2,128,1]{0,2,3,1:T(8,128)(2,1)S(1)} %bitcast.100, f32[2,128]{1,0:T(2,128)S(1)} %fusion.16, f32[2,128,7,128]{1,3,2,0:T(8,128)S(1)} %get-tuple-element.37, f32[2,128]{1,0:T(2,128)S(1)} %get-tuple-element.36), kind=kOutput, calls=%fused_computation.77 | convolution fusion | flops 59637760 | bytes 2361344 | tf_op jit(solution)/shard_map/shtmu,sthc->msuhc/dot_general | solution.py:101
  62.7 2.5 %collective-permute-start.8 = (bf16[2,1,128,2,128]{2,4,0,3,1:T(8,128)(2,1)}, bf16[2,1,128,2,128]{2,4,0,3,1:T(8,128)(2,1)S(1)}, u32[]{:S(2)}, u32[]{:S(2)}) collective-permute-start(bf16[2,1,128,2,128]{2,4,0,3,1:T(8,128)(2,1)} %pad_maximum_fusion.2), channel_id=1, source_target_pairs={{0,32},{16,48},{32,0},{48,16},{64,96},{80,112},{96,64},{112,80},{1... | collective-permute-start | bytes 393224 | tf_op jit(solution)/shard_map/ppermute | solution.py:22
  65.8 6.4 %collective-permute-start.9 = (bf16[2,1,128,2,128]{2,4,0,3,1:T(8,128)(2,1)}, bf16[2,1,128,2,128]{2,4,0,3,1:T(8,128)(2,1)}, u32[]{:S(2)}, u32[]{:S(2)}) collective-permute-start(bf16[2,1,128,2,128]{2,4,0,3,1:T(8,128)(2,1)} %pad_maximum_fusion.3), channel_id=1, source_target_pairs={{0,64},{16,80},{32,96},{48,112},{64,0},{80,16},{96,32},{112,48},{1... | collective-permute-start | bytes 393224 | tf_op jit(solution)/shard_map/ppermute | solution.py:22
  72.9 1.9 %collective-permute-start.10 = (bf16[2,1,128,2,128]{2,4,0,3,1:T(8,128)(2,1)}, bf16[2,1,128,2,128]{2,4,0,3,1:T(8,128)(2,1)}, u32[]{:S(2)}, u32[]{:S(2)}) collective-permute-start(bf16[2,1,128,2,128]{2,4,0,3,1:T(8,128)(2,1)} %pad_maximum_fusion.4), channel_id=1, source_target_pairs={{0,128},{16,144},{32,160},{48,176},{64,192},{80,208},{96,224},{112... | collective-permute-start | bytes 393224 | tf_op jit(solution)/shard_map/ppermute | solution.py:22
  75.5 2.0 %collective-permute-start.11 = (bf16[2,1,128,2,128]{2,4,0,3,1:T(8,128)(2,1)}, bf16[2,1,128,2,128]{2,4,0,3,1:T(8,128)(2,1)}, u32[]{:S(2)}, u32[]{:S(2)}) collective-permute-start(bf16[2,1,128,2,128]{2,4,0,3,1:T(8,128)(2,1)} %pad_maximum_fusion.5), channel_id=1, source_target_pairs={{0,256},{16,272},{32,288},{48,304},{64,320},{80,336},{96,352},{112... | collective-permute-start | bytes 393224 | tf_op jit(solution)/shard_map/ppermute | solution.py:22
  78.1 6.6 %collective-permute-start.12 = (bf16[2,1,128,2,128]{2,4,0,3,1:T(8,128)(2,1)}, bf16[2,1,128,2,128]{2,4,0,3,1:T(8,128)(2,1)}, u32[]{:S(2)}, u32[]{:S(2)}) collective-permute-start(bf16[2,1,128,2,128]{2,4,0,3,1:T(8,128)(2,1)} %pad_maximum_fusion.6), channel_id=1, source_target_pairs={{0,512},{16,528},{32,544},{48,560},{64,576},{80,592},{96,608},{112... | collective-permute-start | bytes 393224 | tf_op jit(solution)/shard_map/ppermute | solution.py:22
  85.4 6.2 %all-to-all-done = bf16[8,8,64,128]{3,2,0,1:T(8,128)(2,1)S(1)} async-done(((bf16[8,8,64,128]{3,2,0,1:T(8,128)(2,1)}), bf16[8,8,64,128]{3,2,0,1:T(8,128)(2,1)S(1)}, u32[]{:S(2)}, u32[]{:S(2)}) %all-to-all-start) | async-done | bytes 1048608 | tf_op jit(solution)/shard_map/all_to_all | solution.py:86
  92.4 4.9 %all-to-all-start.1 = ((bf16[8,64,128]{2,1,0:T(8,128)(2,1)}), bf16[8,64,128]{2,1,0:T(8,128)(2,1)S(1)}, u32[]{:S(2)}, u32[]{:S(2)}) async-start(bf16[8,64,128]{2,1,0:T(8,128)(2,1)} %reduce_sum.41), calls=%async_computation.1 | async-start | bytes 262144 | tf_op jit(solution)/shard_map/all_to_all | solution.py:88
  97.3 1.9 %collective-permute-start.7 = (bf16[2,1,128,2,128]{2,4,0,3,1:T(8,128)(2,1)}, bf16[2,1,128,2,128]{2,4,0,3,1:T(8,128)(2,1)S(1)}, u32[]{:S(2)}, u32[]{:S(2)}) collective-permute-start(bf16[2,1,128,2,128]{2,4,0,3,1:T(8,128)(2,1)} %pad_maximum_fusion.1), channel_id=1, source_target_pairs={{0,16},{16,0},{32,48},{48,32},{64,80},{80,64},{96,112},{112,96},{1... | collective-permute-start | bytes 393224 | tf_op jit(solution)/shard_map/ppermute | solution.py:22
  100.4 4.0 %collective-permute-done.7 = bf16[2,1,128,2,128]{2,4,0,3,1:T(8,128)(2,1)S(1)} collective-permute-done((bf16[2,1,128,2,128]{2,4,0,3,1:T(8,128)(2,1)}, bf16[2,1,128,2,128]{2,4,0,3,1:T(8,128)(2,1)S(1)}, u32[]{:S(2)}, u32[]{:S(2)}) %collective-permute-start.7) | collective-permute-done | bytes 131104 | tf_op jit(solution)/shard_map/ppermute | solution.py:22
  104.4 1.2 %fusion.25 = (bf16[1,1,128,2,128]{2,4,0,3,1:T(8,128)(2,1)S(1)}, bf16[1,1,128,2,128]{2,4,0,3,1:T(8,128)(2,1)S(1)}) fusion(f32[7,1,128,2,128]{2,4,0,3,1:T(8,128)} %get-tuple-element.39, bf16[2,1,128,2,128]{2,4,0,3,1:T(8,128)(2,1)} %collective-permute-done.12, bf16[2,1,128,2,128]{2,4,0,3,1:T(8,128)(2,1)} %collective-permute-done.11, ...), kind=kLoop, calls=%fused_computation.39 | loop fusion | flops 851968 | bytes 1179648 | tf_op jit(solution)/shard_map/convert_element_type | solution.py:115
  107.1 1.6 %all-to-all-done.1 = bf16[8,64,128]{2,1,0:T(8,128)(2,1)S(1)} async-done(((bf16[8,64,128]{2,1,0:T(8,128)(2,1)}), bf16[8,64,128]{2,1,0:T(8,128)(2,1)S(1)}, u32[]{:S(2)}, u32[]{:S(2)}) %all-to-all-start.1) | async-done | bytes 131104 | tf_op jit(solution)/shard_map/all_to_all | solution.py:88
  (62 shorter events, 17.2 us)
Async XLA Ops:
  2.6 31.2 %collective-permute-start.5 = (bf16[2,1,128,256]{2,3,0,1:T(8,128)(2,1)S(1)}, bf16[2,1,128,256]{2,3,0,1:T(8,128)(2,1)S(1)}, u32[]{:S(2)}, u32[]{:S(2)}) collective-permute-start(bf16[2,1,128,256]{2,3,0,1:T(8,128)(2,1)S(1)} %pad_maximum_fusion), channel_id=1, source_target_pairs={{0,512},{16,528},{32,544},{48,560},{64,576},{80,592},{96,608},{112... | collective-permute-start | bytes 393224 | tf_op jit(solution)/shard_map/ppermute | solution.py:22
  13.5 25.1 %collective-permute-start.4 = (bf16[2,1,128,256]{2,3,0,1:T(8,128)(2,1)S(1)}, bf16[2,1,128,256]{2,3,0,1:T(8,128)(2,1)S(1)}, u32[]{:S(2)}, u32[]{:S(2)}) collective-permute-start(bf16[2,1,128,256]{2,3,0,1:T(8,128)(2,1)S(1)} %pad_maximum_fusion), channel_id=1, source_target_pairs={{0,256},{16,272},{32,288},{48,304},{64,320},{80,336},{96,352},{112... | collective-permute-start | bytes 393224 | tf_op jit(solution)/shard_map/ppermute | solution.py:22
  19.6 21.0 %collective-permute-start.3 = (bf16[2,1,128,256]{2,3,0,1:T(8,128)(2,1)S(1)}, bf16[2,1,128,256]{2,3,0,1:T(8,128)(2,1)S(1)}, u32[]{:S(2)}, u32[]{:S(2)}) collective-permute-start(bf16[2,1,128,256]{2,3,0,1:T(8,128)(2,1)S(1)} %pad_maximum_fusion), channel_id=1, source_target_pairs={{0,128},{16,144},{32,160},{48,176},{64,192},{80,208},{96,224},{112... | collective-permute-start | bytes 393224 | tf_op jit(solution)/shard_map/ppermute | solution.py:22
  23.9 19.3 %collective-permute-start.2 = (bf16[2,1,128,256]{2,3,0,1:T(8,128)(2,1)S(1)}, bf16[2,1,128,256]{2,3,0,1:T(8,128)(2,1)S(1)}, u32[]{:S(2)}, u32[]{:S(2)}) collective-permute-start(bf16[2,1,128,256]{2,3,0,1:T(8,128)(2,1)S(1)} %pad_maximum_fusion), channel_id=1, source_target_pairs={{0,64},{16,80},{32,96},{48,112},{64,0},{80,16},{96,32},{112,48},{1... | collective-permute-start | bytes 393224 | tf_op jit(solution)/shard_map/ppermute | solution.py:22
  28.9 14.4 %collective-permute-start.1 = (bf16[2,1,128,256]{2,3,0,1:T(8,128)(2,1)S(1)}, bf16[2,1,128,256]{2,3,0,1:T(8,128)(2,1)S(1)}, u32[]{:S(2)}, u32[]{:S(2)}) collective-permute-start(bf16[2,1,128,256]{2,3,0,1:T(8,128)(2,1)S(1)} %pad_maximum_fusion), channel_id=1, source_target_pairs={{0,32},{16,48},{32,0},{48,16},{64,96},{80,112},{96,64},{112,80},{1... | collective-permute-start | bytes 393224 | tf_op jit(solution)/shard_map/ppermute | solution.py:22
  33.7 9.8 %collective-permute-start = (bf16[2,1,128,256]{2,3,0,1:T(8,128)(2,1)S(1)}, bf16[2,1,128,256]{2,3,0,1:T(8,128)(2,1)S(1)}, u32[]{:S(2)}, u32[]{:S(2)}) collective-permute-start(bf16[2,1,128,256]{2,3,0,1:T(8,128)(2,1)S(1)} %pad_maximum_fusion), channel_id=1, source_target_pairs={{0,16},{16,0},{32,48},{48,32},{64,80},{80,64},{96,112},{112,96},{1... | collective-permute-start | bytes 393224 | tf_op jit(solution)/shard_map/ppermute | solution.py:22
  38.6 9.2 %collective-permute-start.13 = (bf16[128,4096]{1,0:T(8,128)(2,1)}, bf16[128,4096]{1,0:T(8,128)(2,1)}, u32[]{:S(2)}, u32[]{:S(2)}) collective-permute-start(bf16[128,4096]{1,0:T(8,128)(2,1)} %bitcast.14), channel_id=1, source_target_pairs={{0,1},{1,0},{2,3},{3,2},{4,5},{5,4},{6,7},{7,6},{8,9},{9,8},{10,11... | collective-permute-start | bytes 3145736 | tf_op jit(solution)/shard_map/ppermute | solution.py:22
  40.6 15.6 %collective-permute-start.6 = (bf16[256,2048]{1,0:T(8,128)(2,1)}, bf16[256,2048]{1,0:T(8,128)(2,1)}, u32[]{:S(2)}, u32[]{:S(2)}) collective-permute-start(bf16[256,2048]{1,0:T(8,128)(2,1)} %param.10), channel_id=1, source_target_pairs={{0,1},{1,0},{2,3},{3,2},{4,5},{5,4},{6,7},{7,6},{8,9},{9,8},{10,11... | collective-permute-start | bytes 3145736 | tf_op jit(solution)/shard_map/ppermute | solution.py:22
  44.7 3.1 %collective-permute-start.14 = (bf16[128,128]{0,1:T(8,128)(2,1)S(1)}, bf16[128,128]{0,1:T(8,128)(2,1)S(1)}, u32[]{:S(2)}, u32[]{:S(2)}) collective-permute-start(bf16[128,128]{0,1:T(8,128)(2,1)S(1)} %get-tuple-element.35), channel_id=1, source_target_pairs={{0,1},{1,0},{2,3},{3,2},{4,5},{5,4},{6,7},{7,6},{8,9},{9,8},{10,11... | collective-permute-start | bytes 98312 | tf_op jit(solution)/shard_map/ppermute | solution.py:22
  51.1 40.4 %all-to-all-start = ((bf16[8,8,64,128]{3,2,0,1:T(8,128)(2,1)}), bf16[8,8,64,128]{3,2,0,1:T(8,128)(2,1)S(1)}, u32[]{:S(2)}, u32[]{:S(2)}) async-start(bf16[8,8,64,128]{3,2,0,1:T(8,128)(2,1)} %copy.92), calls=%async_computation | async-start | bytes 2097152 | tf_op jit(solution)/shard_map/all_to_all | solution.py:86
  62.7 34.7 %collective-permute-start.8 = (bf16[2,1,128,2,128]{2,4,0,3,1:T(8,128)(2,1)}, bf16[2,1,128,2,128]{2,4,0,3,1:T(8,128)(2,1)S(1)}, u32[]{:S(2)}, u32[]{:S(2)}) collective-permute-start(bf16[2,1,128,2,128]{2,4,0,3,1:T(8,128)(2,1)} %pad_maximum_fusion.2), channel_id=1, source_target_pairs={{0,32},{16,48},{32,0},{48,16},{64,96},{80,112},{96,64},{112,80},{1... | collective-permute-start | bytes 393224 | tf_op jit(solution)/shard_map/ppermute | solution.py:22
  65.8 34.5 %collective-permute-start.9 = (bf16[2,1,128,2,128]{2,4,0,3,1:T(8,128)(2,1)}, bf16[2,1,128,2,128]{2,4,0,3,1:T(8,128)(2,1)}, u32[]{:S(2)}, u32[]{:S(2)}) collective-permute-start(bf16[2,1,128,2,128]{2,4,0,3,1:T(8,128)(2,1)} %pad_maximum_fusion.3), channel_id=1, source_target_pairs={{0,64},{16,80},{32,96},{48,112},{64,0},{80,16},{96,32},{112,48},{1... | collective-permute-start | bytes 393224 | tf_op jit(solution)/shard_map/ppermute | solution.py:22
  72.9 27.5 %collective-permute-start.10 = (bf16[2,1,128,2,128]{2,4,0,3,1:T(8,128)(2,1)}, bf16[2,1,128,2,128]{2,4,0,3,1:T(8,128)(2,1)}, u32[]{:S(2)}, u32[]{:S(2)}) collective-permute-start(bf16[2,1,128,2,128]{2,4,0,3,1:T(8,128)(2,1)} %pad_maximum_fusion.4), channel_id=1, source_target_pairs={{0,128},{16,144},{32,160},{48,176},{64,192},{80,208},{96,224},{112... | collective-permute-start | bytes 393224 | tf_op jit(solution)/shard_map/ppermute | solution.py:22
  75.5 24.9 %collective-permute-start.11 = (bf16[2,1,128,2,128]{2,4,0,3,1:T(8,128)(2,1)}, bf16[2,1,128,2,128]{2,4,0,3,1:T(8,128)(2,1)}, u32[]{:S(2)}, u32[]{:S(2)}) collective-permute-start(bf16[2,1,128,2,128]{2,4,0,3,1:T(8,128)(2,1)} %pad_maximum_fusion.5), channel_id=1, source_target_pairs={{0,256},{16,272},{32,288},{48,304},{64,320},{80,336},{96,352},{112... | collective-permute-start | bytes 393224 | tf_op jit(solution)/shard_map/ppermute | solution.py:22
  78.1 22.3 %collective-permute-start.12 = (bf16[2,1,128,2,128]{2,4,0,3,1:T(8,128)(2,1)}, bf16[2,1,128,2,128]{2,4,0,3,1:T(8,128)(2,1)}, u32[]{:S(2)}, u32[]{:S(2)}) collective-permute-start(bf16[2,1,128,2,128]{2,4,0,3,1:T(8,128)(2,1)} %pad_maximum_fusion.6), channel_id=1, source_target_pairs={{0,512},{16,528},{32,544},{48,560},{64,576},{80,592},{96,608},{112... | collective-permute-start | bytes 393224 | tf_op jit(solution)/shard_map/ppermute | solution.py:22
  92.4 16.4 %all-to-all-start.1 = ((bf16[8,64,128]{2,1,0:T(8,128)(2,1)}), bf16[8,64,128]{2,1,0:T(8,128)(2,1)S(1)}, u32[]{:S(2)}, u32[]{:S(2)}) async-start(bf16[8,64,128]{2,1,0:T(8,128)(2,1)} %reduce_sum.41), calls=%async_computation.1 | async-start | bytes 262144 | tf_op jit(solution)/shard_map/all_to_all | solution.py:88
  97.3 7.1 %collective-permute-start.7 = (bf16[2,1,128,2,128]{2,4,0,3,1:T(8,128)(2,1)}, bf16[2,1,128,2,128]{2,4,0,3,1:T(8,128)(2,1)S(1)}, u32[]{:S(2)}, u32[]{:S(2)}) collective-permute-start(bf16[2,1,128,2,128]{2,4,0,3,1:T(8,128)(2,1)} %pad_maximum_fusion.1), channel_id=1, source_target_pairs={{0,16},{16,0},{32,48},{48,32},{64,80},{80,64},{96,112},{112,96},{1... | collective-permute-start | bytes 393224 | tf_op jit(solution)/shard_map/ppermute | solution.py:22
